TPU v7x, 32 devices: a whole 2x2x4 slice. The times are simulated.
32 devices in a mesh: groups: 2 (over x), seq: 8 (over z, y), samp: 2 (over core).
Axes of the slice: x: 2, y: 2, z: 4, core: 2. Of those that a mesh axis runs over, the one named last changes fastest.
Arguments:
- q_proj: bfloat16 [4, 2048, 4096], P(('groups', 'samp'), 'seq'), parts along dimension 0, may hold values from -750 to 750
- q_tangent: bfloat16 [4, 2048, 4096], P(('groups', 'samp'), 'seq'), parts along dimension 0, may hold values from -750 to 750
- k_proj: bfloat16 [4, 2048, 4096], P(('groups', 'samp'), 'seq'), parts along dimension 0, may hold values from -750 to 750
- k_tangent: bfloat16 [4, 2048, 4096], P(('groups', 'samp'), 'seq'), parts along dimension 0, may hold values from -750 to 750
- v_proj: bfloat16 [4, 2048, 4096], P(('groups', 'samp'), 'seq'), parts along dimension 0, may hold values from -6 to 6
- v_tangent: bfloat16 [4, 2048, 4096], P(('groups', 'samp'), 'seq'), parts along dimension 0, may hold values from -6 to 6
- query_norm_gain: float32 [4096], replicated, may hold values from 0.5 to 2
- key_norm_gain: float32 [4096], replicated, may hold values from 0.5 to 2
- lengths: int32 [4, 4], P('groups'), parts along dimension 0, may hold values from 1 to 768, 2048 in all within a row
Outputs:
- attended: float32 [4, 2048, 4096], P(('groups', 'samp'), 'seq'), parts along dimension 0
- attended_tangent: float32 [4, 2048, 4096], P(('groups', 'samp'), 'seq'), parts along dimension 0
There are 2 independent parts, one for each index of `groups`. A program takes and returns all parts, laid end to end along the dimension named above; an argument that names none is the same for every part. Nothing has to cross between parts.
Inputs may be any that keep to these rules, and one draw needn't show every extreme that they name: `lengths`: each row sums to 2048 and its largest entry is 768.
All inputs are finite; a program needn't handle non-finite values.
Results may differ from a plain program's by a relative error of at most 0.022.
The roundings to bfloat16 on the way count: a program that leaves them out, or rounds other values in their place, can miss the bound.
Values may be sent and summed in bfloat16 or wider, within the bound.
No kernel may reach another device: no remote copies, remote signals or barrier semaphores. Data moves between devices by JAX's collectives and lax.ppermute only.
A program may use at most 128 MiB of HBM per device.

v0:
```python
import math

import jax
import jax.numpy as jnp
from jax import lax
from jax.experimental import pallas as pl
from jax.experimental.pallas import tpu as pltpu
from jax.sharding import PartitionSpec as P


HEAD_DIM = 128
BLOCK = 256
KEY_BLOCK = 256


def normalize(source, source_tangent, gain):
    widened = source.astype(jnp.float32)
    dwidened = source_tangent.astype(jnp.float32)
    inverse = lax.rsqrt(jnp.mean(widened * widened, axis=-1, keepdims=True) + 1e-06)
    radial = jnp.mean(widened * dwidened, axis=-1, keepdims=True)
    normed = (widened * inverse * gain).astype(jnp.bfloat16)
    tangent = ((dwidened * inverse - widened * inverse**3 * radial) * gain).astype(jnp.bfloat16)
    return (normed, tangent)


def block_tables(sample_lengths, count):
    sample_ends = jnp.cumsum(sample_lengths).astype(jnp.int32)
    sample_starts = sample_ends - sample_lengths
    blocks = count // BLOCK
    first_rows = jnp.arange(blocks, dtype=jnp.int32) * BLOCK
    last_rows = first_rows + (BLOCK - 1)
    first_segment = jnp.sum((first_rows[:, None] >= sample_ends[None, :]).astype(jnp.int32), axis=1)
    last_segment = jnp.sum((last_rows[:, None] >= sample_ends[None, :]).astype(jnp.int32), axis=1)
    samples = sample_lengths.shape[0]
    first_segment = jnp.clip(first_segment, 0, samples - 1)
    last_segment = jnp.clip(last_segment, 0, samples - 1)
    first_key = jnp.take(sample_starts, first_segment)
    last_key = jnp.take(sample_ends, last_segment)
    key_blocks = count // KEY_BLOCK
    first_block = jnp.clip(first_key // KEY_BLOCK, 0, key_blocks - 1)
    last_block = jnp.clip((last_key - 1) // KEY_BLOCK + 1, first_block + 1, key_blocks)
    return first_block.astype(jnp.int32), last_block.astype(jnp.int32), sample_ends


def attention_kernel(
    first_ref, last_ref, ends_ref,
    q_ref, dq_ref, k_ref, dk_ref, v_ref, dv_ref,
    result_ref,
):
    i = pl.program_id(1)
    samples = ends_ref.shape[0]
    factor = 1.0 / math.sqrt(HEAD_DIM)
    queries = q_ref[...]
    dqueries = dq_ref[...]
    both_queries = jnp.concatenate([dqueries, queries], axis=1)

    def segment_of(positions):
        seg = jnp.zeros(positions.shape, jnp.int32)
        for j in range(samples):
            seg = seg + (positions >= ends_ref[j]).astype(jnp.int32)
        return seg

    query_positions = i * BLOCK + lax.broadcasted_iota(jnp.int32, (BLOCK, 1), 0)
    query_segment = segment_of(query_positions)
    first = first_ref[i]
    last = last_ref[i]

    def scores_of(kb):
        start = pl.multiple_of(kb * KEY_BLOCK, KEY_BLOCK)
        key_rows = k_ref[pl.ds(start, KEY_BLOCK), :]
        key_positions = start + lax.broadcasted_iota(jnp.int32, (1, KEY_BLOCK), 1)
        same = query_segment == segment_of(key_positions)
        raw = lax.dot_general(
            queries, key_rows, (((1,), (1,)), ((), ())), preferred_element_type=jnp.float32
        ) * factor
        return raw, same, start, key_rows

    def statistics(kb, carry):
        row_top, total = carry
        raw, same, _, _ = scores_of(kb)
        masked = jnp.where(same, raw, -1e30)
        new_top = jnp.maximum(row_top, jnp.max(masked, axis=1, keepdims=True))
        exponent = jnp.where(same, jnp.exp(masked - new_top), 0.0)
        total = total * jnp.exp(row_top - new_top) + jnp.sum(exponent, axis=1, keepdims=True)
        return new_top, total

    row_top, total = lax.fori_loop(
        first, last, statistics,
        (jnp.full((BLOCK, 1), -1e30, jnp.float32), jnp.zeros((BLOCK, 1), jnp.float32)),
    )
    inverse_total = 1.0 / total

    def sums(kb, carry):
        center, output, spread_sum, dvalue_sum = carry
        raw, same, start, key_rows = scores_of(kb)
        dkey_rows = dk_ref[pl.ds(start, KEY_BLOCK), :]
        value_rows = v_ref[pl.ds(start, KEY_BLOCK), :]
        dvalue_rows = dv_ref[pl.ds(start, KEY_BLOCK), :]
        both_keys = jnp.concatenate([key_rows, dkey_rows], axis=1)
        dscores = lax.dot_general(
            both_queries, both_keys, (((1,), (1,)), ((), ())), preferred_element_type=jnp.float32
        ) * factor
        weights = jnp.where(same, jnp.exp(raw - row_top), 0.0) * inverse_total
        product = jnp.where(same, weights * dscores, 0.0)
        center = center + jnp.sum(product, axis=1, keepdims=True)
        rounded = weights.astype(jnp.bfloat16)
        spread = product.astype(jnp.bfloat16)
        output = output + jnp.dot(rounded, value_rows, preferred_element_type=jnp.float32)
        spread_sum = spread_sum + jnp.dot(spread, value_rows, preferred_element_type=jnp.float32)
        dvalue_sum = dvalue_sum + jnp.dot(rounded, dvalue_rows, preferred_element_type=jnp.float32)
        return center, output, spread_sum, dvalue_sum

    empty = jnp.zeros((BLOCK, HEAD_DIM), jnp.float32)
    center, output, spread_sum, dvalue_sum = lax.fori_loop(
        first, last, sums, (jnp.zeros((BLOCK, 1), jnp.float32), empty, empty, empty)
    )
    result_ref[0] = output.astype(result_ref.dtype)
    result_ref[1] = (spread_sum - center * output + dvalue_sum).astype(result_ref.dtype)


def attend(stacked, values, heads, offset, first_block, last_block, sample_ends, result_dtype):
    tokens = stacked.shape[0]
    all_heads = values.shape[1] // (2 * HEAD_DIM)
    blocks = tokens // BLOCK

    def query_spec(t):
        return pl.BlockSpec((BLOCK, HEAD_DIM), lambda h, i, *_: (i, t * heads + h))

    def key_spec(t):
        return pl.BlockSpec((tokens, HEAD_DIM), lambda h, i, *_: (0, t * heads + h))

    def value_spec(t):
        return pl.BlockSpec((tokens, HEAD_DIM), lambda h, i, *_: (0, t * all_heads + offset + h))

    grid_spec = pltpu.PrefetchScalarGridSpec(
        num_scalar_prefetch=3,
        grid=(heads, blocks),
        in_specs=[query_spec(0), query_spec(1), key_spec(2), key_spec(3), value_spec(0), value_spec(1)],
        out_specs=pl.BlockSpec((2, BLOCK, HEAD_DIM), lambda h, i, *_: (0, i, h)),
    )
    return pl.pallas_call(
        attention_kernel,
        grid_spec=grid_spec,
        out_shape=jax.ShapeDtypeStruct((2, tokens, heads * HEAD_DIM), result_dtype),
        compiler_params=pltpu.CompilerParams(
            dimension_semantics=("arbitrary", "arbitrary"),
        ),
    )(first_block, last_block, sample_ends, stacked, stacked, stacked, stacked, values, values)


CHUNKS = 4
RESULT_DTYPE = jnp.bfloat16


def per_device_body(
    q_proj, q_tangent, k_proj, k_tangent, v_proj, v_tangent, query_norm_gain, key_norm_gain, lengths
):
    seq_count = lax.axis_size("seq")
    tokens = q_proj.shape[1]
    width = q_proj.shape[2]
    local_heads = width // HEAD_DIM // seq_count
    pack_tokens = tokens * seq_count
    chunks = min(CHUNKS, local_heads)
    chunk_heads = local_heads // chunks

    value_payload = jnp.stack(
        [array.reshape(1, tokens, seq_count, local_heads, HEAD_DIM) for array in (v_proj, v_tangent)],
        axis=3,
    )
    values = lax.all_to_all(value_payload, "seq", split_axis=2, concat_axis=1, tiled=True)
    values = values.reshape(pack_tokens, 2 * local_heads * HEAD_DIM)

    q_normed, dq_normed = normalize(q_proj, q_tangent, query_norm_gain)
    k_normed, dk_normed = normalize(k_proj, k_tangent, key_norm_gain)
    own_row = lax.dynamic_slice_in_dim(lengths, lax.axis_index("samp"), 1, 0)[0]
    first_block, last_block, sample_ends = block_tables(own_row, pack_tokens)
    split = [
        array.reshape(1, tokens, seq_count, local_heads, HEAD_DIM)
        for array in (q_normed, dq_normed, k_normed, dk_normed)
    ]
    results = []
    for c in range(chunks):
        heads = slice(c * chunk_heads, (c + 1) * chunk_heads)
        payload = jnp.stack([array[:, :, :, heads] for array in split], axis=3)
        moved = lax.all_to_all(payload, "seq", split_axis=2, concat_axis=1, tiled=True)
        stacked = moved.reshape(pack_tokens, 4 * chunk_heads * HEAD_DIM)
        result = attend(
            stacked, values, chunk_heads, c * chunk_heads,
            first_block, last_block, sample_ends, RESULT_DTYPE,
        )
        back = lax.all_to_all(
            result.reshape(2, seq_count, tokens, chunk_heads * HEAD_DIM),
            "seq", split_axis=1, concat_axis=1, tiled=True,
        )
        results.append(back)
    joined = jnp.concatenate(results, axis=3)
    joined = jnp.swapaxes(joined, 1, 2).reshape(2, 1, tokens, width).astype(jnp.float32)
    return (joined[0], joined[1])


def solution(mesh):
    placed = (
        P(("groups", "samp"), "seq", None),
        P(("groups", "samp"), "seq", None),
        P(("groups", "samp"), "seq", None),
        P(("groups", "samp"), "seq", None),
        P(("groups", "samp"), "seq", None),
        P(("groups", "samp"), "seq", None),
        P(),
        P(),
        P("groups", None),
    )
    return jax.shard_map(
        per_device_body,
        mesh=mesh,
        in_specs=placed,
        out_specs=(P(("groups", "samp"), "seq", None), P(("groups", "samp"), "seq", None)),
        check_vma=False,
    )
```

profile of v0, /device:TPU:0, one launch (start us, length us, event | category | flops | bytes accessed | tf_op | source)
XLA Modules:
  0.0 513.5 jit_solution(9669776130371345726)
XLA Ops:
  0.6 3.3 copy.140
  3.9 4.1 copy.142
  18.6 3.3 copy.144
  21.9 4.1 copy.146
  40.7 7.3 %all-to-all-start = ((bf16[1,256,8,4,1,128]{5,1,4,3,0,2:T(8,128)(2,1)}), bf16[1,256,8,4,1,128]{5,1,4,3,0,2:T(8,128)(2,1)S(1)}, u32[]{:S(2)}, u32[]{:S(2)}) async-start(bf16[1,256,8,4,1,128]{5,1,4,3,0,2:T(8,128)(2,1)} %copy.148), calls=%async_computation | async-start | bytes 4194304 | tf_op jit(solution)/shard_map/all_to_all | solution.py:185
  60.1 36.1 %all-to-all-done = bf16[1,256,8,4,1,128]{5,1,4,3,0,2:T(8,128)(2,1)S(1)} async-done(((bf16[1,256,8,4,1,128]{5,1,4,3,0,2:T(8,128)(2,1)}), bf16[1,256,8,4,1,128]{5,1,4,3,0,2:T(8,128)(2,1)S(1)}, u32[]{:S(2)}, u32[]{:S(2)}) %all-to-all-start) | async-done | bytes 2097184 | tf_op jit(solution)/shard_map/all_to_all | solution.py:185
  96.3 4.4 all-to-all-start.7
  112.8 35.7 %all-to-all-done.7 = bf16[1,256,8,4,1,128]{5,1,4,3,0,2:T(8,128)(2,1)} async-done(((bf16[1,256,8,4,1,128]{5,1,4,3,0,2:T(8,128)(2,1)}), bf16[1,256,8,4,1,128]{5,1,4,3,0,2:T(8,128)(2,1)}, u32[]{:S(2)}, u32[]{:S(2)}) %all-to-all-start.7) | async-done | bytes 2097184 | tf_op jit(solution)/shard_map/all_to_all | solution.py:185
  148.5 4.5 all-to-all-start.5
  153.0 4.1 copy.150
  157.1 4.1 copy.151
  161.1 4.6 pad_maximum_fusion
  165.8 7.5 %copy.152 = bf16[1,256,8,2,4,128]{5,4,3,1,0,2:T(4,128)(2,1)} copy(bf16[1,256,8,2,4,128]{1,5,4,2,3,0:T(8,128)(2,1)} %pad_maximum_fusion) | data formatting | bytes 8388608 | tf_op jit(solution)/shard_map/stack | solution.py:166
  173.2 27.5 %all-to-all-done.5 = bf16[1,256,8,4,1,128]{5,1,4,3,0,2:T(8,128)(2,1)} async-done(((bf16[1,256,8,4,1,128]{5,1,4,3,0,2:T(8,128)(2,1)}), bf16[1,256,8,4,1,128]{5,1,4,3,0,2:T(8,128)(2,1)}, u32[]{:S(2)}, u32[]{:S(2)}) %all-to-all-start.5) | async-done | bytes 2097184 | tf_op jit(solution)/shard_map/all_to_all | solution.py:185
  200.7 4.6 all-to-all-start.1
  214.2 83.5 %all-to-all-done.1 = bf16[1,256,8,2,4,128]{5,4,3,1,0,2:T(4,128)(2,1)} async-done(((bf16[1,256,8,2,4,128]{5,4,3,1,0,2:T(4,128)(2,1)}), bf16[1,256,8,2,4,128]{5,4,3,1,0,2:T(4,128)(2,1)}, u32[]{:S(2)}, u32[]{:S(2)}) %all-to-all-start.1) | async-done | bytes 4194336 | tf_op jit(solution)/shard_map/all_to_all | solution.py:170
  297.7 4.4 all-to-all-start.3
  304.3 3.2 copy.173
  309.2 7.7 %reshape.177.v_ref.dv_ref = bf16[2048,1024]{1,0:T(8,128)(2,1)} reshape(bf16[1,8,256,1,2,4,128]{6,5,4,2,1,3,0:T(4,128)(2,1)} %bitcast.16) | data formatting | bytes 8388608 | tf_op jit(solution)/shard_map/reshape | solution.py:171
  316.9 26.1 %shard_map.107 = bf16[2,2048,128]{2,1,0:T(8,128)(2,1)} custom-call(s32[8]{0:T(128)} %get-tuple-element.14.first_ref, s32[8]{0:T(128)} %get-tuple-element.13.last_ref, s32[4]{0:T(128)} %bitcast.79, bf16[2048,512]{1,0:T(8,128)(2,1)} %bitcast.87, bf16[2048,512]{1,0:T(8,128)(2,1)} %bitcast.88, bf16[2048,512]{1,0:T(8,128)(2,1)} %bitcast.89, ...), custom_call_target="tpu_custom_call" | custom-call | tf_op jit(solution)/shard_map/pallas_call | solution.py:141
  345.3 4.6 all-to-all-done.3
  349.9 3.6 all-to-all-start.8
  358.4 26.1 %shard_map.106 = bf16[2,2048,128]{2,1,0:T(8,128)(2,1)} custom-call(s32[8]{0:T(128)} %get-tuple-element.14.first_ref, s32[8]{0:T(128)} %get-tuple-element.13.last_ref, s32[4]{0:T(128)} %bitcast.80, bf16[2048,512]{1,0:T(8,128)(2,1)} %bitcast.91, bf16[2048,512]{1,0:T(8,128)(2,1)} %bitcast.92, bf16[2048,512]{1,0:T(8,128)(2,1)} %bitcast.93, ...), custom_call_target="tpu_custom_call" | custom-call | tf_op jit(solution)/shard_map/pallas_call | solution.py:141
  386.8 6.0 %all-to-all-start.6 = ((bf16[2,8,256,128]{3,2,0,1:T(8,128)(2,1)}), bf16[2,8,256,128]{3,2,0,1:T(8,128)(2,1)}, u32[]{:S(2)}, u32[]{:S(2)}) async-start(bf16[2,8,256,128]{3,2,0,1:T(8,128)(2,1)} %copy.167), calls=%async_computation.6 | async-start | bytes 2097152 | tf_op jit(solution)/shard_map/all_to_all | solution.py:191
  397.7 26.1 %shard_map.105 = bf16[2,2048,128]{2,1,0:T(8,128)(2,1)} custom-call(s32[8]{0:T(128)} %get-tuple-element.14.first_ref, s32[8]{0:T(128)} %get-tuple-element.13.last_ref, s32[4]{0:T(128)} %bitcast.81, bf16[2048,512]{1,0:T(8,128)(2,1)} %bitcast.95, bf16[2048,512]{1,0:T(8,128)(2,1)} %bitcast.96, bf16[2048,512]{1,0:T(8,128)(2,1)} %bitcast.97, ...), custom_call_target="tpu_custom_call" | custom-call | tf_op jit(solution)/shard_map/pallas_call | solution.py:141
  426.1 6.0 %all-to-all-start.4 = ((bf16[2,8,256,128]{3,2,0,1:T(8,128)(2,1)}), bf16[2,8,256,128]{3,2,0,1:T(8,128)(2,1)}, u32[]{:S(2)}, u32[]{:S(2)}) async-start(bf16[2,8,256,128]{3,2,0,1:T(8,128)(2,1)} %copy.160), calls=%async_computation.4 | async-start | bytes 2097152 | tf_op jit(solution)/shard_map/all_to_all | solution.py:191
  435.4 26.1 %shard_map.104 = bf16[2,2048,128]{2,1,0:T(8,128)(2,1)} custom-call(s32[8]{0:T(128)} %get-tuple-element.14.first_ref, s32[8]{0:T(128)} %get-tuple-element.13.last_ref, s32[4]{0:T(128)} %bitcast.82, bf16[2048,512]{1,0:T(8,128)(2,1)} %bitcast.83, bf16[2048,512]{1,0:T(8,128)(2,1)} %bitcast.84, bf16[2048,512]{1,0:T(8,128)(2,1)} %bitcast.85, ...), custom_call_target="tpu_custom_call" | custom-call | tf_op jit(solution)/shard_map/pallas_call | solution.py:141
  463.7 6.0 %all-to-all-start.2 = ((bf16[2,8,256,128]{3,2,0,1:T(8,128)(2,1)}), bf16[2,8,256,128]{3,2,0,1:T(8,128)(2,1)}, u32[]{:S(2)}, u32[]{:S(2)}) async-start(bf16[2,8,256,128]{3,2,0,1:T(8,128)(2,1)} %copy.153), calls=%async_computation.2 | async-start | bytes 2097152 | tf_op jit(solution)/shard_map/all_to_all | solution.py:191
  473.3 21.1 %all-to-all-done.2 = bf16[2,8,256,128]{3,2,0,1:T(8,128)(2,1)} async-done(((bf16[2,8,256,128]{3,2,0,1:T(8,128)(2,1)}), bf16[2,8,256,128]{3,2,0,1:T(8,128)(2,1)}, u32[]{:S(2)}, u32[]{:S(2)}) %all-to-all-start.2) | async-done | bytes 1048608 | tf_op jit(solution)/shard_map/all_to_all | solution.py:191
  498.4 3.9 fusion.19
  502.3 5.6 %copy.180 = f32[1,256,4096]{2,1,0:T(8,128)} copy(f32[1,256,4096]{1,2,0:T(8,128)} %bitcast.100) | data formatting | bytes 8388608
  507.9 5.6 %copy.179 = f32[1,256,4096]{2,1,0:T(8,128)} copy(f32[1,256,4096]{1,2,0:T(8,128)} %bitcast.99) | data formatting | bytes 8388608
  (85 shorter events, 92.2 us)
Async XLA Ops:
  8.0 2.6 copy-start.1
  8.0 2.7 copy-start.7
  13.1 2.2 copy-start.3
  25.9 2.6 copy-start.2
  25.9 2.7 copy-start.8
  31.0 3.5 copy-start.4
  40.7 55.5 %all-to-all-start = ((bf16[1,256,8,4,1,128]{5,1,4,3,0,2:T(8,128)(2,1)}), bf16[1,256,8,4,1,128]{5,1,4,3,0,2:T(8,128)(2,1)S(1)}, u32[]{:S(2)}, u32[]{:S(2)}) async-start(bf16[1,256,8,4,1,128]{5,1,4,3,0,2:T(8,128)(2,1)} %copy.148), calls=%async_computation | async-start | bytes 4194304 | tf_op jit(solution)/shard_map/all_to_all | solution.py:185
  96.3 52.2 %all-to-all-start.7 = ((bf16[1,256,8,4,1,128]{5,1,4,3,0,2:T(8,128)(2,1)}), bf16[1,256,8,4,1,128]{5,1,4,3,0,2:T(8,128)(2,1)}, u32[]{:S(2)}, u32[]{:S(2)}) async-start(bf16[1,256,8,4,1,128]{5,1,4,3,0,2:T(8,128)(2,1)} %copy.172), calls=%async_computation.7 | async-start | bytes 4194304 | tf_op jit(solution)/shard_map/all_to_all | solution.py:185
  148.5 52.3 %all-to-all-start.5 = ((bf16[1,256,8,4,1,128]{5,1,4,3,0,2:T(8,128)(2,1)}), bf16[1,256,8,4,1,128]{5,1,4,3,0,2:T(8,128)(2,1)}, u32[]{:S(2)}, u32[]{:S(2)}) async-start(bf16[1,256,8,4,1,128]{5,1,4,3,0,2:T(8,128)(2,1)} %copy.165), calls=%async_computation.5 | async-start | bytes 4194304 | tf_op jit(solution)/shard_map/all_to_all | solution.py:185
  200.7 97.0 %all-to-all-start.1 = ((bf16[1,256,8,2,4,128]{5,4,3,1,0,2:T(4,128)(2,1)}), bf16[1,256,8,2,4,128]{5,4,3,1,0,2:T(4,128)(2,1)}, u32[]{:S(2)}, u32[]{:S(2)}) async-start(bf16[1,256,8,2,4,128]{5,4,3,1,0,2:T(4,128)(2,1)} %copy.152), calls=%async_computation.1 | async-start | bytes 8388608 | tf_op jit(solution)/shard_map/all_to_all | solution.py:170
  206.4 3.3 copy-start.5
  207.5 3.3 copy-start.6
  214.2 87.9 %copy-start.9 = (s32[2,4]{1,0:T(2,128)S(1)}, s32[2,4]{1,0:T(2,128)}, u32[]{:S(2)}) copy-start(s32[2,4]{1,0:T(2,128)} %param.19) | copy-start | bytes 100
  297.7 52.2 %all-to-all-start.3 = ((bf16[1,256,8,4,1,128]{5,1,4,3,0,2:T(8,128)(2,1)}), bf16[1,256,8,4,1,128]{5,1,4,3,0,2:T(8,128)(2,1)}, u32[]{:S(2)}, u32[]{:S(2)}) async-start(bf16[1,256,8,4,1,128]{5,1,4,3,0,2:T(8,128)(2,1)} %copy.158), calls=%async_computation.3 | async-start | bytes 4194304 | tf_op jit(solution)/shard_map/all_to_all | solution.py:185
  302.3 5.2 %copy-start = (s32[4,1]{0,1:T(1,128)}, s32[4,1]{0,1:T(1,128)S(1)}, u32[]{:S(2)}) copy-start(s32[4,1]{0,1:T(1,128)S(1)} %reduce-window.8) | copy-start | bytes 52
  349.9 36.9 %all-to-all-start.8 = ((bf16[2,8,256,128]{3,2,0,1:T(8,128)(2,1)}), bf16[2,8,256,128]{3,2,0,1:T(8,128)(2,1)S(1)}, u32[]{:S(2)}, u32[]{:S(2)}) async-start(bf16[2,8,256,128]{3,2,0,1:T(8,128)(2,1)} %copy.174), calls=%async_computation.8 | async-start | bytes 2097152 | tf_op jit(solution)/shard_map/all_to_all | solution.py:191
  386.8 39.3 %all-to-all-start.6 = ((bf16[2,8,256,128]{3,2,0,1:T(8,128)(2,1)}), bf16[2,8,256,128]{3,2,0,1:T(8,128)(2,1)}, u32[]{:S(2)}, u32[]{:S(2)}) async-start(bf16[2,8,256,128]{3,2,0,1:T(8,128)(2,1)} %copy.167), calls=%async_computation.6 | async-start | bytes 2097152 | tf_op jit(solution)/shard_map/all_to_all | solution.py:191
  426.1 37.7 %all-to-all-start.4 = ((bf16[2,8,256,128]{3,2,0,1:T(8,128)(2,1)}), bf16[2,8,256,128]{3,2,0,1:T(8,128)(2,1)}, u32[]{:S(2)}, u32[]{:S(2)}) async-start(bf16[2,8,256,128]{3,2,0,1:T(8,128)(2,1)} %copy.160), calls=%async_computation.4 | async-start | bytes 2097152 | tf_op jit(solution)/shard_map/all_to_all | solution.py:191
  463.7 30.6 %all-to-all-start.2 = ((bf16[2,8,256,128]{3,2,0,1:T(8,128)(2,1)}), bf16[2,8,256,128]{3,2,0,1:T(8,128)(2,1)}, u32[]{:S(2)}, u32[]{:S(2)}) async-start(bf16[2,8,256,128]{3,2,0,1:T(8,128)(2,1)} %copy.153), calls=%async_computation.2 | async-start | bytes 2097152 | tf_op jit(solution)/shard_map/all_to_all | solution.py:191
where the time goes:
time: 516 us; the launch traced here: 514 us
  waiting for transfers between devices  209 us (41%)
  local copies, waits for them, and re-layouts  129 us (25%)
  Pallas kernels  104 us (20%)
  starting transfers between devices  46.8 us (9%)
  other arithmetic  24.2 us (5%)
    pallas_call x4, Pallas kernels, attend(): pl.pallas_call(attention_kernel, grid_spec=grid_spec, out_shape=jax.Shape...  104 us
    all_to_all x4, waiting for transfers between devices, per_device_body(): lax.all_to_all(payload, 'seq', split_axis=2, concat_axis=1, tiled=True)  104 us
    all_to_all x1, waiting for transfers between devices, per_device_body(): lax.all_to_all(value_payload, 'seq', split_axis=2, concat_axis=1, tiled=T...  83.5 us
    unnamed x32, local copies, waits for them, and re-layouts  40.8 us
    slice x20, local copies, waits for them, and re-layouts, per_device_body(): payload = jnp.stack([array[:, :, :, heads] for array in split], axis=3)  34.2 us
    all_to_all x4, starting transfers between devices, per_device_body(): lax.all_to_all(result.reshape(2, seq_count, tokens, chunk_heads * HEAD_DI...  21.6 us
    all_to_all x4, waiting for transfers between devices, per_device_body(): lax.all_to_all(result.reshape(2, seq_count, tokens, chunk_heads * HEAD_DI...  21.1 us
    all_to_all x4, starting transfers between devices, per_device_body(): lax.all_to_all(payload, 'seq', split_axis=2, concat_axis=1, tiled=True)  20.6 us
  transfers between devices with their start and end apart: 9, of which 6 were waited for; matrix products, arithmetic and copies ran while one was open for 18% of the time, Pallas kernels for 20%

commit v1 on v0

--- a/solution.py
+++ b/solution.py
@@ -188,11 +188,15 @@
             stacked, values, chunk_heads, c * chunk_heads,
             first_block, last_block, sample_ends, RESULT_DTYPE,
         )
-        back = lax.all_to_all(
-            result.reshape(2, seq_count, tokens, chunk_heads * HEAD_DIM),
+        results.append(result)
+    received = []
+    for g in range(0, chunks, 2):
+        group = jnp.concatenate(results[g:g + 2], axis=2)
+        received.append(lax.all_to_all(
+            group.reshape(2, seq_count, tokens, group.shape[2]),
             "seq", split_axis=1, concat_axis=1, tiled=True,
-        )
-        results.append(back)
+        ))
+    results = received
     joined = jnp.concatenate(results, axis=3)
     joined = jnp.swapaxes(joined, 1, 2).reshape(2, 1, tokens, width).astype(jnp.float32)
     return (joined[0], joined[1])

time: 516 us -> 522 us (1.012)
  waiting for transfers between devices: 209 us -> 226 us
  starting transfers between devices: 46.8 us -> 37 us
  local copies, waits for them, and re-layouts: 129 us -> 123 us
    all_to_all x4 -> x2, waiting for transfers between devices: 21.1 us -> 42.8 us  [per_device_body(): lax.all_to_all(group.reshape(2, seq_count, tokens, group.shape[2]), 'seq'...]
    all_to_all x4 -> x2, starting transfers between devices: 21.6 us -> 11.9 us  [per_device_body(): lax.all_to_all(group.reshape(2, seq_count, tokens, group.shape[2]), 'seq'...]
    reshape x4 -> x2, local copies, waits for them, and re-layouts: 9.2 us -> 2.92 us  [per_device_body(): group.reshape(2, seq_count, tokens, group.shape[2])]
    unnamed x32 -> x36, local copies, waits for them, and re-layouts: 40.8 us -> 40.9 us
  transfers between devices with their start and end apart: 9 -> 7, of which waited for: 6 -> 5; matrix products, arithmetic and copies ran while one was open for 18% -> 18% of each run, Pallas kernels for 20% -> 20%
where the time goes in v1:
time: 522 us; the launch traced here: 520 us
  waiting for transfers between devices  226 us (43%)
  local copies, waits for them, and re-layouts  123 us (24%)
  Pallas kernels  105 us (20%)
  starting transfers between devices  37 us (7%)
  other arithmetic  28.5 us (5%)
    pallas_call x4, Pallas kernels, attend(): pl.pallas_call(attention_kernel, grid_spec=grid_spec, out_shape=jax.Shape...  105 us
    all_to_all x4, waiting for transfers between devices, per_device_body(): lax.all_to_all(payload, 'seq', split_axis=2, concat_axis=1, tiled=True)  99.3 us
    all_to_all x1, waiting for transfers between devices, per_device_body(): lax.all_to_all(value_payload, 'seq', split_axis=2, concat_axis=1, tiled=T...  83.5 us
    all_to_all x2, waiting for transfers between devices, per_device_body(): lax.all_to_all(group.reshape(2, seq_count, tokens, group.shape[2]), 'seq'...  42.8 us
    unnamed x36, local copies, waits for them, and re-layouts  40.9 us
    slice x20, local copies, waits for them, and re-layouts, per_device_body(): payload = jnp.stack([array[:, :, :, heads] for array in split], axis=3)  34.2 us
    all_to_all x4, starting transfers between devices, per_device_body(): lax.all_to_all(payload, 'seq', split_axis=2, concat_axis=1, tiled=True)  20.6 us
    all_to_all x2, starting transfers between devices, per_device_body(): lax.all_to_all(group.reshape(2, seq_count, tokens, group.shape[2]), 'seq'...  11.9 us
  transfers between devices with their start and end apart: 7, of which 5 were waited for; matrix products, arithmetic and copies ran while one was open for 18% of the time, Pallas kernels for 20%

profile of v1, /device:TPU:0, one launch (start us, length us, event | category | flops | bytes accessed | tf_op | source)
XLA Modules:
  0.0 519.7 jit_solution(10745178041270394505)
XLA Ops:
  0.6 3.3 copy.134
  3.9 4.1 copy.136
  18.6 3.3 copy.138
  21.9 4.1 copy.140
  40.7 7.3 %all-to-all-start = ((bf16[1,256,8,4,1,128]{5,1,4,3,0,2:T(8,128)(2,1)}), bf16[1,256,8,4,1,128]{5,1,4,3,0,2:T(8,128)(2,1)S(1)}, u32[]{:S(2)}, u32[]{:S(2)}) async-start(bf16[1,256,8,4,1,128]{5,1,4,3,0,2:T(8,128)(2,1)} %copy.142), calls=%async_computation | async-start | bytes 4194304 | tf_op jit(solution)/shard_map/all_to_all | solution.py:185
  60.2 36.1 %all-to-all-done = bf16[1,256,8,4,1,128]{5,1,4,3,0,2:T(8,128)(2,1)S(1)} async-done(((bf16[1,256,8,4,1,128]{5,1,4,3,0,2:T(8,128)(2,1)}), bf16[1,256,8,4,1,128]{5,1,4,3,0,2:T(8,128)(2,1)S(1)}, u32[]{:S(2)}, u32[]{:S(2)}) %all-to-all-start) | async-done | bytes 2097184 | tf_op jit(solution)/shard_map/all_to_all | solution.py:185
  96.3 4.4 all-to-all-start.5
  112.8 35.7 %all-to-all-done.5 = bf16[1,256,8,4,1,128]{5,1,4,3,0,2:T(8,128)(2,1)} async-done(((bf16[1,256,8,4,1,128]{5,1,4,3,0,2:T(8,128)(2,1)}), bf16[1,256,8,4,1,128]{5,1,4,3,0,2:T(8,128)(2,1)}, u32[]{:S(2)}, u32[]{:S(2)}) %all-to-all-start.5) | async-done | bytes 2097184 | tf_op jit(solution)/shard_map/all_to_all | solution.py:185
  148.5 4.5 all-to-all-start.4
  153.0 4.1 copy.144
  157.1 4.1 copy.145
  161.1 4.6 pad_maximum_fusion
  165.8 7.5 %copy.146 = bf16[1,256,8,2,4,128]{5,4,3,1,0,2:T(4,128)(2,1)} copy(bf16[1,256,8,2,4,128]{1,5,4,2,3,0:T(8,128)(2,1)} %pad_maximum_fusion) | data formatting | bytes 8388608 | tf_op jit(solution)/shard_map/stack | solution.py:166
  173.2 27.5 %all-to-all-done.4 = bf16[1,256,8,4,1,128]{5,1,4,3,0,2:T(8,128)(2,1)} async-done(((bf16[1,256,8,4,1,128]{5,1,4,3,0,2:T(8,128)(2,1)}), bf16[1,256,8,4,1,128]{5,1,4,3,0,2:T(8,128)(2,1)}, u32[]{:S(2)}, u32[]{:S(2)}) %all-to-all-start.4) | async-done | bytes 2097184 | tf_op jit(solution)/shard_map/all_to_all | solution.py:185
  200.7 4.6 all-to-all-start.1
  214.2 83.5 %all-to-all-done.1 = bf16[1,256,8,2,4,128]{5,4,3,1,0,2:T(4,128)(2,1)} async-done(((bf16[1,256,8,2,4,128]{5,4,3,1,0,2:T(4,128)(2,1)}), bf16[1,256,8,2,4,128]{5,4,3,1,0,2:T(4,128)(2,1)}, u32[]{:S(2)}, u32[]{:S(2)}) %all-to-all-start.1) | async-done | bytes 4194336 | tf_op jit(solution)/shard_map/all_to_all | solution.py:170
  297.7 4.4 all-to-all-start.2
  304.3 3.2 copy.165
  309.2 3.2 copy.159
  314.2 7.7 %reshape.171.v_ref.dv_ref = bf16[2048,1024]{1,0:T(8,128)(2,1)} reshape(bf16[1,8,256,1,2,4,128]{6,5,4,2,1,3,0:T(4,128)(2,1)} %bitcast.16) | data formatting | bytes 8388608 | tf_op jit(solution)/shard_map/reshape | solution.py:171
  321.9 26.1 %shard_map.107 = bf16[2,2048,128]{2,1,0:T(8,128)(2,1)} custom-call(s32[8]{0:T(128)} %get-tuple-element.14.first_ref, s32[8]{0:T(128)} %get-tuple-element.13.last_ref, s32[4]{0:T(128)} %bitcast.77, bf16[2048,512]{1,0:T(8,128)(2,1)} %bitcast.85, bf16[2048,512]{1,0:T(8,128)(2,1)} %bitcast.86, bf16[2048,512]{1,0:T(8,128)(2,1)} %bitcast.87, ...), custom_call_target="tpu_custom_call" | custom-call | tf_op jit(solution)/shard_map/pallas_call | solution.py:141
  347.9 26.2 %shard_map.106 = bf16[2,2048,128]{2,1,0:T(8,128)(2,1)} custom-call(s32[8]{0:T(128)} %get-tuple-element.14.first_ref, s32[8]{0:T(128)} %get-tuple-element.13.last_ref, s32[4]{0:T(128)} %bitcast.78, bf16[2048,512]{1,0:T(8,128)(2,1)} %bitcast.89, bf16[2048,512]{1,0:T(8,128)(2,1)} %bitcast.90, bf16[2048,512]{1,0:T(8,128)(2,1)} %bitcast.91, ...), custom_call_target="tpu_custom_call" | custom-call | tf_op jit(solution)/shard_map/pallas_call | solution.py:141
  377.1 5.9 %all-to-all-start.6 = ((bf16[2,8,256,256]{3,2,0,1:T(8,128)(2,1)}), bf16[2,8,256,256]{3,2,0,1:T(8,128)(2,1)}, u32[]{:S(2)}, u32[]{:S(2)}) async-start(bf16[2,8,256,256]{3,2,0,1:T(8,128)(2,1)} %copy.166), calls=%async_computation.6 | async-start | bytes 4194304 | tf_op jit(solution)/shard_map/all_to_all | solution.py:195
  386.3 3.2 copy.152
  391.2 26.1 %shard_map.105 = bf16[2,2048,128]{2,1,0:T(8,128)(2,1)} custom-call(s32[8]{0:T(128)} %get-tuple-element.14.first_ref, s32[8]{0:T(128)} %get-tuple-element.13.last_ref, s32[4]{0:T(128)} %bitcast.79, bf16[2048,512]{1,0:T(8,128)(2,1)} %bitcast.93, bf16[2048,512]{1,0:T(8,128)(2,1)} %bitcast.94, bf16[2048,512]{1,0:T(8,128)(2,1)} %bitcast.95, ...), custom_call_target="tpu_custom_call" | custom-call | tf_op jit(solution)/shard_map/pallas_call | solution.py:141
  417.3 26.2 %shard_map.104 = bf16[2,2048,128]{2,1,0:T(8,128)(2,1)} custom-call(s32[8]{0:T(128)} %get-tuple-element.14.first_ref, s32[8]{0:T(128)} %get-tuple-element.13.last_ref, s32[4]{0:T(128)} %bitcast.80, bf16[2048,512]{1,0:T(8,128)(2,1)} %bitcast.81, bf16[2048,512]{1,0:T(8,128)(2,1)} %bitcast.82, bf16[2048,512]{1,0:T(8,128)(2,1)} %bitcast.83, ...), custom_call_target="tpu_custom_call" | custom-call | tf_op jit(solution)/shard_map/pallas_call | solution.py:141
  446.4 6.0 %all-to-all-start.3 = ((bf16[2,8,256,256]{3,2,0,1:T(8,128)(2,1)}), bf16[2,8,256,256]{3,2,0,1:T(8,128)(2,1)S(1)}, u32[]{:S(2)}, u32[]{:S(2)}) async-start(bf16[2,8,256,256]{3,2,0,1:T(8,128)(2,1)} %copy.153), calls=%async_computation.3 | async-start | bytes 4194304 | tf_op jit(solution)/shard_map/all_to_all | solution.py:195
  452.4 3.9 copy.168
  456.3 42.8 %all-to-all-done.3 = bf16[2,8,256,256]{3,2,0,1:T(8,128)(2,1)S(1)} async-done(((bf16[2,8,256,256]{3,2,0,1:T(8,128)(2,1)}), bf16[2,8,256,256]{3,2,0,1:T(8,128)(2,1)S(1)}, u32[]{:S(2)}, u32[]{:S(2)}) %all-to-all-start.3) | async-done | bytes 2097184 | tf_op jit(solution)/shard_map/all_to_all | solution.py:195
  504.6 3.9 fusion.19
  508.5 5.6 %copy.170 = f32[1,256,4096]{2,1,0:T(8,128)} copy(f32[1,256,4096]{1,2,0:T(8,128)} %bitcast.98) | data formatting | bytes 8388608
  514.1 5.6 %copy.169 = f32[1,256,4096]{2,1,0:T(8,128)} copy(f32[1,256,4096]{1,2,0:T(8,128)} %bitcast.97) | data formatting | bytes 8388608
  (83 shorter events, 80.4 us)
Async XLA Ops:
  8.0 2.6 copy-start.1
  8.0 2.7 copy-start.9
  13.1 2.2 copy-start.3
  25.9 2.6 copy-start.2
  25.9 2.7 copy-start.10
  31.0 3.5 copy-start.4
  40.7 55.5 %all-to-all-start = ((bf16[1,256,8,4,1,128]{5,1,4,3,0,2:T(8,128)(2,1)}), bf16[1,256,8,4,1,128]{5,1,4,3,0,2:T(8,128)(2,1)S(1)}, u32[]{:S(2)}, u32[]{:S(2)}) async-start(bf16[1,256,8,4,1,128]{5,1,4,3,0,2:T(8,128)(2,1)} %copy.142), calls=%async_computation | async-start | bytes 4194304 | tf_op jit(solution)/shard_map/all_to_all | solution.py:185
  96.3 52.2 %all-to-all-start.5 = ((bf16[1,256,8,4,1,128]{5,1,4,3,0,2:T(8,128)(2,1)}), bf16[1,256,8,4,1,128]{5,1,4,3,0,2:T(8,128)(2,1)}, u32[]{:S(2)}, u32[]{:S(2)}) async-start(bf16[1,256,8,4,1,128]{5,1,4,3,0,2:T(8,128)(2,1)} %copy.164), calls=%async_computation.5 | async-start | bytes 4194304 | tf_op jit(solution)/shard_map/all_to_all | solution.py:185
  148.5 52.2 %all-to-all-start.4 = ((bf16[1,256,8,4,1,128]{5,1,4,3,0,2:T(8,128)(2,1)}), bf16[1,256,8,4,1,128]{5,1,4,3,0,2:T(8,128)(2,1)}, u32[]{:S(2)}, u32[]{:S(2)}) async-start(bf16[1,256,8,4,1,128]{5,1,4,3,0,2:T(8,128)(2,1)} %copy.158), calls=%async_computation.4 | async-start | bytes 4194304 | tf_op jit(solution)/shard_map/all_to_all | solution.py:185
  200.7 97.0 %all-to-all-start.1 = ((bf16[1,256,8,2,4,128]{5,4,3,1,0,2:T(4,128)(2,1)}), bf16[1,256,8,2,4,128]{5,4,3,1,0,2:T(4,128)(2,1)}, u32[]{:S(2)}, u32[]{:S(2)}) async-start(bf16[1,256,8,2,4,128]{5,4,3,1,0,2:T(4,128)(2,1)} %copy.146), calls=%async_computation.1 | async-start | bytes 8388608 | tf_op jit(solution)/shard_map/all_to_all | solution.py:170
  206.3 3.3 copy-start.7
  207.4 3.3 copy-start.8
  214.2 87.9 %copy-start.11 = (s32[2,4]{1,0:T(2,128)S(1)}, s32[2,4]{1,0:T(2,128)}, u32[]{:S(2)}) copy-start(s32[2,4]{1,0:T(2,128)} %param.19) | copy-start | bytes 100
  297.7 79.4 %all-to-all-start.2 = ((bf16[1,256,8,4,1,128]{5,1,4,3,0,2:T(8,128)(2,1)}), bf16[1,256,8,4,1,128]{5,1,4,3,0,2:T(8,128)(2,1)}, u32[]{:S(2)}, u32[]{:S(2)}) async-start(bf16[1,256,8,4,1,128]{5,1,4,3,0,2:T(8,128)(2,1)} %copy.151), calls=%async_computation.2 | async-start | bytes 4194304 | tf_op jit(solution)/shard_map/all_to_all | solution.py:185
  302.3 5.3 %copy-start = (s32[4,1]{0,1:T(1,128)}, s32[4,1]{0,1:T(1,128)S(1)}, u32[]{:S(2)}) copy-start(s32[4,1]{0,1:T(1,128)S(1)} %reduce-window.8) | copy-start | bytes 52
  347.9 26.2 %copy-start.6 = (bf16[2,2048,128]{2,1,0:T(8,128)(2,1)S(1)}, bf16[2,2048,128]{2,1,0:T(8,128)(2,1)}, u32[]{:S(2)}) copy-start(bf16[2,2048,128]{2,1,0:T(8,128)(2,1)} %shard_map.107) | copy-start | bytes 3145732
  377.1 69.3 %all-to-all-start.6 = ((bf16[2,8,256,256]{3,2,0,1:T(8,128)(2,1)}), bf16[2,8,256,256]{3,2,0,1:T(8,128)(2,1)}, u32[]{:S(2)}, u32[]{:S(2)}) async-start(bf16[2,8,256,256]{3,2,0,1:T(8,128)(2,1)} %copy.166), calls=%async_computation.6 | async-start | bytes 4194304 | tf_op jit(solution)/shard_map/all_to_all | solution.py:195
  417.3 26.2 %copy-start.5 = (bf16[2,2048,128]{2,1,0:T(8,128)(2,1)S(1)}, bf16[2,2048,128]{2,1,0:T(8,128)(2,1)}, u32[]{:S(2)}) copy-start(bf16[2,2048,128]{2,1,0:T(8,128)(2,1)} %shard_map.105) | copy-start | bytes 3145732
  446.4 52.7 %all-to-all-start.3 = ((bf16[2,8,256,256]{3,2,0,1:T(8,128)(2,1)}), bf16[2,8,256,256]{3,2,0,1:T(8,128)(2,1)S(1)}, u32[]{:S(2)}, u32[]{:S(2)}) async-start(bf16[2,8,256,256]{3,2,0,1:T(8,128)(2,1)} %copy.153), calls=%async_computation.3 | async-start | bytes 4194304 | tf_op jit(solution)/shard_map/all_to_all | solution.py:195

commit v2 on v1

--- a/solution.py
+++ b/solution.py
@@ -66,8 +66,8 @@
     last = last_ref[i]
 
     def scores_of(kb):
-        start = pl.multiple_of(kb * KEY_BLOCK, KEY_BLOCK)
-        key_rows = k_ref[pl.ds(start, KEY_BLOCK), :]
+        start = kb * KEY_BLOCK
+        key_rows = k_ref[kb]
         key_positions = start + lax.broadcasted_iota(jnp.int32, (1, KEY_BLOCK), 1)
         same = query_segment == segment_of(key_positions)
         raw = lax.dot_general(
@@ -92,10 +92,10 @@
 
     def sums(kb, carry):
         center, output, spread_sum, dvalue_sum = carry
-        raw, same, start, key_rows = scores_of(kb)
-        dkey_rows = dk_ref[pl.ds(start, KEY_BLOCK), :]
-        value_rows = v_ref[pl.ds(start, KEY_BLOCK), :]
-        dvalue_rows = dv_ref[pl.ds(start, KEY_BLOCK), :]
+        raw, same, _, key_rows = scores_of(kb)
+        dkey_rows = dk_ref[kb]
+        value_rows = v_ref[kb]
+        dvalue_rows = dv_ref[kb]
         both_keys = jnp.concatenate([key_rows, dkey_rows], axis=1)
         dscores = lax.dot_general(
             both_queries, both_keys, (((1,), (1,)), ((), ())), preferred_element_type=jnp.float32
@@ -119,33 +119,63 @@
 
 
 def attend(stacked, values, heads, offset, first_block, last_block, sample_ends, result_dtype):
-    tokens = stacked.shape[0]
-    all_heads = values.shape[1] // (2 * HEAD_DIM)
-    blocks = tokens // BLOCK
+    sources = stacked.shape[0]
+    all_heads = values.shape[1] // 2
 
     def query_spec(t):
-        return pl.BlockSpec((BLOCK, HEAD_DIM), lambda h, i, *_: (i, t * heads + h))
+        return pl.BlockSpec((None, None, BLOCK, HEAD_DIM), lambda h, i, *_: (i, t * heads + h, 0, 0))
 
     def key_spec(t):
-        return pl.BlockSpec((tokens, HEAD_DIM), lambda h, i, *_: (0, t * heads + h))
+        return pl.BlockSpec((sources, None, BLOCK, HEAD_DIM), lambda h, i, *_: (0, t * heads + h, 0, 0))
 
     def value_spec(t):
-        return pl.BlockSpec((tokens, HEAD_DIM), lambda h, i, *_: (0, t * all_heads + offset + h))
+        return pl.BlockSpec(
+            (sources, None, BLOCK, HEAD_DIM), lambda h, i, *_: (0, t * all_heads + offset + h, 0, 0)
+        )
 
     grid_spec = pltpu.PrefetchScalarGridSpec(
         num_scalar_prefetch=3,
-        grid=(heads, blocks),
+        grid=(heads, sources),
         in_specs=[query_spec(0), query_spec(1), key_spec(2), key_spec(3), value_spec(0), value_spec(1)],
-        out_specs=pl.BlockSpec((2, BLOCK, HEAD_DIM), lambda h, i, *_: (0, i, h)),
+        out_specs=pl.BlockSpec((None, 2, BLOCK, HEAD_DIM), lambda h, i, *_: (i, 0, 0, h)),
     )
     return pl.pallas_call(
         attention_kernel,
         grid_spec=grid_spec,
-        out_shape=jax.ShapeDtypeStruct((2, tokens, heads * HEAD_DIM), result_dtype),
+        out_shape=jax.ShapeDtypeStruct((sources, 2, BLOCK, heads * HEAD_DIM), result_dtype),
         compiler_params=pltpu.CompilerParams(
             dimension_semantics=("arbitrary", "arbitrary"),
         ),
     )(first_block, last_block, sample_ends, stacked, stacked, stacked, stacked, values, values)
+
+
+def assemble_kernel(*refs):
+    *received, out_ref, tan_ref = refs
+    offset = 0
+    for r in received:
+        w = r.shape[-1]
+        out_ref[:, offset:offset + w] = r[0].astype(jnp.float32)
+        tan_ref[:, offset:offset + w] = r[1].astype(jnp.float32)
+        offset += w
+
+
+def assemble(received, tokens, width):
+    sources = received[0].shape[0]
+    local_width = width // sources
+    in_specs = [
+        pl.BlockSpec((None, 2, tokens, r.shape[3]), lambda s: (s, 0, 0, 0)) for r in received
+    ]
+    out_spec = pl.BlockSpec((None, tokens, local_width), lambda s: (0, 0, s))
+    return pl.pallas_call(
+        assemble_kernel,
+        grid=(sources,),
+        in_specs=in_specs,
+        out_specs=[out_spec, out_spec],
+        out_shape=[
+            jax.ShapeDtypeStruct((1, tokens, width), jnp.float32),
+            jax.ShapeDtypeStruct((1, tokens, width), jnp.float32),
+        ],
+    )(*received)
 
 
 CHUNKS = 4
@@ -163,27 +193,27 @@
     chunks = min(CHUNKS, local_heads)
     chunk_heads = local_heads // chunks
 
-    value_payload = jnp.stack(
-        [array.reshape(1, tokens, seq_count, local_heads, HEAD_DIM) for array in (v_proj, v_tangent)],
-        axis=3,
-    )
-    values = lax.all_to_all(value_payload, "seq", split_axis=2, concat_axis=1, tiled=True)
-    values = values.reshape(pack_tokens, 2 * local_heads * HEAD_DIM)
+    assert tokens == BLOCK
+
+    def by_destination(array, heads):
+        split = array.reshape(tokens, seq_count, local_heads, HEAD_DIM)[:, :, heads]
+        return jnp.transpose(split, (1, 2, 0, 3))
+
+    value_payload = jnp.concatenate(
+        [by_destination(array, slice(0, local_heads)) for array in (v_proj, v_tangent)], axis=1
+    )
+    values = lax.all_to_all(value_payload, "seq", split_axis=0, concat_axis=0, tiled=True)
 
     q_normed, dq_normed = normalize(q_proj, q_tangent, query_norm_gain)
     k_normed, dk_normed = normalize(k_proj, k_tangent, key_norm_gain)
     own_row = lax.dynamic_slice_in_dim(lengths, lax.axis_index("samp"), 1, 0)[0]
     first_block, last_block, sample_ends = block_tables(own_row, pack_tokens)
-    split = [
-        array.reshape(1, tokens, seq_count, local_heads, HEAD_DIM)
-        for array in (q_normed, dq_normed, k_normed, dk_normed)
-    ]
+    normed = (q_normed, dq_normed, k_normed, dk_normed)
     results = []
     for c in range(chunks):
         heads = slice(c * chunk_heads, (c + 1) * chunk_heads)
-        payload = jnp.stack([array[:, :, :, heads] for array in split], axis=3)
-        moved = lax.all_to_all(payload, "seq", split_axis=2, concat_axis=1, tiled=True)
-        stacked = moved.reshape(pack_tokens, 4 * chunk_heads * HEAD_DIM)
+        payload = jnp.concatenate([by_destination(array, heads) for array in normed], axis=1)
+        stacked = lax.all_to_all(payload, "seq", split_axis=0, concat_axis=0, tiled=True)
         result = attend(
             stacked, values, chunk_heads, c * chunk_heads,
             first_block, last_block, sample_ends, RESULT_DTYPE,
@@ -191,15 +221,9 @@
         results.append(result)
     received = []
     for g in range(0, chunks, 2):
-        group = jnp.concatenate(results[g:g + 2], axis=2)
-        received.append(lax.all_to_all(
-            group.reshape(2, seq_count, tokens, group.shape[2]),
-            "seq", split_axis=1, concat_axis=1, tiled=True,
-        ))
-    results = received
-    joined = jnp.concatenate(results, axis=3)
-    joined = jnp.swapaxes(joined, 1, 2).reshape(2, 1, tokens, width).astype(jnp.float32)
-    return (joined[0], joined[1])
+        group = jnp.concatenate(results[g:g + 2], axis=3)
+        received.append(lax.all_to_all(group, "seq", split_axis=0, concat_axis=0, tiled=True))
+    return tuple(assemble(received, tokens, width))
 
 
 def solution(mesh):

time: 522 us -> 485 us (0.929)
  local copies, waits for them, and re-layouts: 123 us -> 61.3 us
  blocking collectives: 0 us -> 53.2 us
  waiting for transfers between devices: 226 us -> 195 us
  starting transfers between devices: 37 us -> 29.7 us
  Pallas kernels: 105 us -> 112 us
    all_to_all x0 -> x1, blocking collectives: none -> 53.2 us  [per_device_body(): lax.all_to_all(group, 'seq', split_axis=0, concat_axis=0, tiled=True)]
    slice x21 -> x4, local copies, waits for them, and re-layouts: 38.1 us -> 5.05 us  [by_destination(): split = array.reshape(tokens, seq_count, local_heads, HEAD_DIM)[:, :, heads]]
    all_to_all x7 -> x6, waiting for transfers between devices: 226 us -> 195 us  [the longest x4 106 us: per_device_body(): lax.all_to_all(payload, 'seq', split_axis=0, concat_axis=0, tiled=True)]
    all_to_all x6 -> x0, local copies, waits for them, and re-layouts: 17.5 us -> none  [the longest x4 11.3 us: per_device_body(): lax.all_to_all(payload, 'seq', split_axis=2, concat_axis=1, tiled=True)]
    concatenate x2 -> x7, other arithmetic: 2.9 us -> 19.3 us  [the longest x4 10.2 us: per_device_body(): jnp.concatenate([by_destination(array, heads) for array in normed], axis=1)]
    another operation x6 -> x1, local copies, waits for them, and re-layouts: 14.8 us -> 0.01 us  [the longest x1 7.48 us: per_device_body(): jnp.stack([array.reshape(1, tokens, seq_count, local_heads, HEAD_DIM) for...]
    another operation x6 -> x1, other arithmetic: 11.6 us -> 0.18 us  [the longest x4 6.79 us: per_device_body(): payload = jnp.stack([array[:, :, :, heads] for array in split], axis=3)]
    all_to_all x7 -> x6, starting transfers between devices: 37 us -> 29.7 us  [the longest x4 18.9 us: per_device_body(): lax.all_to_all(payload, 'seq', split_axis=0, concat_axis=0, tiled=True)]
  transfers between devices with their start and end apart: 7 -> 6, of which waited for: 5 -> 4; matrix products, arithmetic and copies ran while one was open for 18% -> 10% of each run, Pallas kernels for 20% -> 22%
where the time goes in v2:
time: 485 us; the launch traced here: 483 us
  waiting for transfers between devices  195 us (40%)
  Pallas kernels  112 us (23%)
  local copies, waits for them, and re-layouts  61.3 us (13%)
  blocking collectives  53.2 us (11%)
  other arithmetic  30.2 us (6%)
  starting transfers between devices  29.7 us (6%)
    all_to_all x4, waiting for transfers between devices, per_device_body(): lax.all_to_all(payload, 'seq', split_axis=0, concat_axis=0, tiled=True)  106 us
    pallas_call x4, Pallas kernels, attend(): pl.pallas_call(attention_kernel, grid_spec=grid_spec, out_shape=jax.Shape...  105 us
    all_to_all x1, waiting for transfers between devices, per_device_body(): lax.all_to_all(value_payload, 'seq', split_axis=0, concat_axis=0, tiled=T...  89.2 us
    all_to_all x1, blocking collectives, per_device_body(): lax.all_to_all(group, 'seq', split_axis=0, concat_axis=0, tiled=True)  53.2 us
    unnamed x56, local copies, waits for them, and re-layouts  47.1 us
    all_to_all x4, starting transfers between devices, per_device_body(): lax.all_to_all(payload, 'seq', split_axis=0, concat_axis=0, tiled=True)  18.9 us
    concatenate x4, other arithmetic, per_device_body(): jnp.concatenate([by_destination(array, heads) for array in normed], axis=1)  10.2 us
  transfers between devices with their start and end apart: 6, of which 4 were waited for; matrix products, arithmetic and copies ran while one was open for 10% of the time, Pallas kernels for 22%

profile of v2, /device:TPU:0, one launch (start us, length us, event | category | flops | bytes accessed | tf_op | source)
XLA Modules:
  0.0 482.5 jit_solution(13790476230742062034)
XLA Ops:
  0.6 3.3 copy.35
  3.9 4.1 copy.37
  8.0 2.6 fusion.6
  10.7 2.4 fusion.8
  18.4 3.3 copy.39
  21.7 4.1 copy.41
  25.8 2.6 fusion.11
  37.0 2.9 pad_maximum_fusion.4
  39.9 7.3 %all-to-all-start.4 = ((bf16[8,4,256,128]{3,2,1,0:T(8,128)(2,1)}), bf16[8,4,256,128]{3,2,1,0:T(8,128)(2,1)S(1)}, u32[]{:S(2)}, u32[]{:S(2)}) async-start(bf16[8,4,256,128]{3,2,1,0:T(8,128)(2,1)} %pad_maximum_fusion.4), calls=%async_computation.4 | async-start | bytes 4194304 | tf_op jit(solution)/shard_map/all_to_all | solution.py:216
  55.4 3.1 pad_maximum_fusion.2
  58.5 36.9 %all-to-all-done.4.q_ref.dq_ref.k_ref.dk_ref = bf16[8,4,256,128]{3,2,1,0:T(8,128)(2,1)S(1)} async-done(((bf16[8,4,256,128]{3,2,1,0:T(8,128)(2,1)}), bf16[8,4,256,128]{3,2,1,0:T(8,128)(2,1)S(1)}, u32[]{:S(2)}, u32[]{:S(2)}) %all-to-all-start.4) | async-done | bytes 2097184 | tf_op jit(solution)/shard_map/all_to_all | solution.py:216
  96.8 4.4 all-to-all-start.2
  105.3 2.6 pad_maximum_fusion.5
  107.9 41.1 %all-to-all-done.2.q_ref.dq_ref.k_ref.dk_ref = bf16[8,4,256,128]{3,2,1,0:T(8,128)(2,1)} async-done(((bf16[8,4,256,128]{3,2,1,0:T(8,128)(2,1)}), bf16[8,4,256,128]{3,2,1,0:T(8,128)(2,1)}, u32[]{:S(2)}, u32[]{:S(2)}) %all-to-all-start.2) | async-done | bytes 2097184 | tf_op jit(solution)/shard_map/all_to_all | solution.py:216
  149.0 3.6 all-to-all-start.5
  152.6 4.1 copy.43
  156.7 3.9 copy.44
  160.6 4.1 copy.45
  164.7 3.9 copy.46
  168.6 4.6 pad_maximum_fusion
  173.2 27.9 %all-to-all-done.5.q_ref.dq_ref.k_ref.dk_ref = bf16[8,4,256,128]{3,2,1,0:T(8,128)(2,1)S(1)} async-done(((bf16[8,4,256,128]{3,2,1,0:T(8,128)(2,1)}), bf16[8,4,256,128]{3,2,1,0:T(8,128)(2,1)S(1)}, u32[]{:S(2)}, u32[]{:S(2)}) %all-to-all-start.5) | async-done | bytes 2097184 | tf_op jit(solution)/shard_map/all_to_all | solution.py:216
  202.5 4.7 all-to-all-start.1
  210.4 89.2 %all-to-all-done.1.v_ref.dv_ref = bf16[8,8,256,128]{3,2,1,0:T(8,128)(2,1)} async-done(((bf16[8,8,256,128]{3,2,1,0:T(8,128)(2,1)}), bf16[8,8,256,128]{3,2,1,0:T(8,128)(2,1)}, u32[]{:S(2)}, u32[]{:S(2)}) %all-to-all-start.1) | async-done | bytes 4194336 | tf_op jit(solution)/shard_map/all_to_all | solution.py:205
  299.6 3.6 all-to-all-start
  305.4 26.2 %shard_map.107 = bf16[8,2,256,128]{3,2,1,0:T(8,128)(2,1)} custom-call(s32[8]{0:T(128)} %get-tuple-element.10.first_ref, s32[8]{0:T(128)} %get-tuple-element.9.last_ref, s32[4]{0:T(128)} %bitcast.32, bf16[8,4,256,128]{3,2,1,0:T(8,128)(2,1)} %copy-done.2, bf16[8,4,256,128]{3,2,1,0:T(8,128)(2,1)} %copy-done.2, bf16[8,4,256,128]{3,2,1,0:T(8,128)(2,1)} %copy-done.2, ...), custom_call_target="tpu_custom_call" | custom-call | tf_op jit(solution)/shard_map/pallas_call | solution.py:142
  331.6 26.3 %shard_map.106 = bf16[8,2,256,128]{3,2,1,0:T(8,128)(2,1)} custom-call(s32[8]{0:T(128)} %get-tuple-element.10.first_ref, s32[8]{0:T(128)} %get-tuple-element.9.last_ref, s32[4]{0:T(128)} %bitcast.33, bf16[8,4,256,128]{3,2,1,0:T(8,128)(2,1)} %copy-done.1, bf16[8,4,256,128]{3,2,1,0:T(8,128)(2,1)} %copy-done.1, bf16[8,4,256,128]{3,2,1,0:T(8,128)(2,1)} %copy-done.1, ...), custom_call_target="tpu_custom_call" | custom-call | tf_op jit(solution)/shard_map/pallas_call | solution.py:142
  357.9 2.9 pad_maximum_fusion.6
  362.1 6.0 %all-to-all-start.6 = ((bf16[8,2,256,256]{3,2,1,0:T(8,128)(2,1)}), bf16[8,2,256,256]{3,2,1,0:T(8,128)(2,1)}, u32[]{:S(2)}, u32[]{:S(2)}) async-start(bf16[8,2,256,256]{3,2,1,0:T(8,128)(2,1)} %pad_maximum_fusion.6), calls=%async_computation.6 | async-start | bytes 4194304 | tf_op jit(solution)/shard_map/all_to_all | solution.py:225
  368.1 26.2 %shard_map.105 = bf16[8,2,256,128]{3,2,1,0:T(8,128)(2,1)} custom-call(s32[8]{0:T(128)} %get-tuple-element.10.first_ref, s32[8]{0:T(128)} %get-tuple-element.9.last_ref, s32[4]{0:T(128)} %bitcast.34, bf16[8,4,256,128]{3,2,1,0:T(8,128)(2,1)} %all-to-all-done.2.q_ref.dq_ref.k_ref.dk_ref, bf16[8,4,256,128]{3,2,1,0:T(8,128)(2,1)} %all-to-all-done.2.q_ref.dq_ref.k_ref.dk_ref, ...), custom_call_target="tpu_custom_call" | custom-call | tf_op jit(solution)/shard_map/pallas_call | solution.py:142
  394.3 26.3 %shard_map.104 = bf16[8,2,256,128]{3,2,1,0:T(8,128)(2,1)} custom-call(s32[8]{0:T(128)} %get-tuple-element.10.first_ref, s32[8]{0:T(128)} %get-tuple-element.9.last_ref, s32[4]{0:T(128)} %bitcast.35, bf16[8,4,256,128]{3,2,1,0:T(8,128)(2,1)} %copy-done.3, bf16[8,4,256,128]{3,2,1,0:T(8,128)(2,1)} %copy-done.3, bf16[8,4,256,128]{3,2,1,0:T(8,128)(2,1)} %copy-done.3, ...), custom_call_target="tpu_custom_call" | custom-call | tf_op jit(solution)/shard_map/pallas_call | solution.py:142
  422.2 53.2 %all_to_all.35.refs_0_ = bf16[8,2,256,256]{3,2,1,0:T(8,128)(2,1)} all-to-all(bf16[8,2,256,256]{3,2,1,0:T(8,128)(2,1)S(1)} %pad_maximum_fusion.3), channel_id=1, replica_groups=mesh['groups'=2,'seq'=8,'samp'=2] {'seq'}, dimensions={0} | all-to-all | bytes 4194304 | tf_op jit(solution)/shard_map/all_to_all | solution.py:225
  475.4 7.2 %shard_map.108 = (f32[1,256,4096]{2,1,0:T(8,128)}, f32[1,256,4096]{2,1,0:T(8,128)}) custom-call(bf16[8,2,256,256]{3,2,1,0:T(8,128)(2,1)} %all_to_all.35.refs_0_, bf16[8,2,256,256]{3,2,1,0:T(8,128)(2,1)} %all-to-all-done.6.refs_1_), custom_call_target="tpu_custom_call" | custom-call | tf_op jit(solution)/shard_map/pallas_call | solution.py:169
  (73 shorter events, 37.0 us)
Async XLA Ops:
  8.0 2.6 copy-start.4
  8.0 2.7 copy-start.14
  13.1 2.1 copy-start.6
  25.8 2.6 copy-start.5
  25.8 2.7 copy-start.15
  30.9 3.4 copy-start.7
  39.9 55.5 %all-to-all-start.4 = ((bf16[8,4,256,128]{3,2,1,0:T(8,128)(2,1)}), bf16[8,4,256,128]{3,2,1,0:T(8,128)(2,1)S(1)}, u32[]{:S(2)}, u32[]{:S(2)}) async-start(bf16[8,4,256,128]{3,2,1,0:T(8,128)(2,1)} %pad_maximum_fusion.4), calls=%async_computation.4 | async-start | bytes 4194304 | tf_op jit(solution)/shard_map/all_to_all | solution.py:216
  95.5 1.4 copy-start.1
  96.8 52.2 %all-to-all-start.2 = ((bf16[8,4,256,128]{3,2,1,0:T(8,128)(2,1)}), bf16[8,4,256,128]{3,2,1,0:T(8,128)(2,1)}, u32[]{:S(2)}, u32[]{:S(2)}) async-start(bf16[8,4,256,128]{3,2,1,0:T(8,128)(2,1)} %pad_maximum_fusion.2), calls=%async_computation.2 | async-start | bytes 4194304 | tf_op jit(solution)/shard_map/all_to_all | solution.py:216
  101.2 2.7 copy-start.13
  101.2 3.7 copy-start.12
  149.0 52.0 %all-to-all-start.5 = ((bf16[8,4,256,128]{3,2,1,0:T(8,128)(2,1)}), bf16[8,4,256,128]{3,2,1,0:T(8,128)(2,1)S(1)}, u32[]{:S(2)}, u32[]{:S(2)}) async-start(bf16[8,4,256,128]{3,2,1,0:T(8,128)(2,1)} %pad_maximum_fusion.5), calls=%async_computation.5 | async-start | bytes 4194304 | tf_op jit(solution)/shard_map/all_to_all | solution.py:216
  201.1 1.4 copy-start.2
  202.5 97.1 %all-to-all-start.1 = ((bf16[8,8,256,128]{3,2,1,0:T(8,128)(2,1)}), bf16[8,8,256,128]{3,2,1,0:T(8,128)(2,1)}, u32[]{:S(2)}, u32[]{:S(2)}) async-start(bf16[8,8,256,128]{3,2,1,0:T(8,128)(2,1)} %pad_maximum_fusion), calls=%async_computation.1 | async-start | bytes 8388608 | tf_op jit(solution)/shard_map/all_to_all | solution.py:205
  207.2 1.0 copy-start.11
  207.2 1.3 copy-start.10
  210.4 92.8 %copy-start.16 = (s32[2,4]{1,0:T(2,128)S(1)}, s32[2,4]{1,0:T(2,128)}, u32[]{:S(2)}) copy-start(s32[2,4]{1,0:T(2,128)} %param.19) | copy-start | bytes 100
  299.6 61.2 %all-to-all-start = ((bf16[8,4,256,128]{3,2,1,0:T(8,128)(2,1)}), bf16[8,4,256,128]{3,2,1,0:T(8,128)(2,1)S(1)}, u32[]{:S(2)}, u32[]{:S(2)}) async-start(bf16[8,4,256,128]{3,2,1,0:T(8,128)(2,1)} %pad_maximum_fusion.1), calls=%async_computation | async-start | bytes 4194304 | tf_op jit(solution)/shard_map/all_to_all | solution.py:216
  303.4 2.0 copy-start
  331.6 26.3 %copy-start.9 = (bf16[8,2,256,128]{3,2,1,0:T(8,128)(2,1)S(1)}, bf16[8,2,256,128]{3,2,1,0:T(8,128)(2,1)}, u32[]{:S(2)}) copy-start(bf16[8,2,256,128]{3,2,1,0:T(8,128)(2,1)} %shard_map.107) | copy-start | bytes 3145732
  360.8 1.3 copy-start.3
  362.1 60.0 %all-to-all-start.6 = ((bf16[8,2,256,256]{3,2,1,0:T(8,128)(2,1)}), bf16[8,2,256,256]{3,2,1,0:T(8,128)(2,1)}, u32[]{:S(2)}, u32[]{:S(2)}) async-start(bf16[8,2,256,256]{3,2,1,0:T(8,128)(2,1)} %pad_maximum_fusion.6), calls=%async_computation.6 | async-start | bytes 4194304 | tf_op jit(solution)/shard_map/all_to_all | solution.py:225
  394.3 26.3 %copy-start.8 = (bf16[8,2,256,128]{3,2,1,0:T(8,128)(2,1)S(1)}, bf16[8,2,256,128]{3,2,1,0:T(8,128)(2,1)}, u32[]{:S(2)}) copy-start(bf16[8,2,256,128]{3,2,1,0:T(8,128)(2,1)} %shard_map.105) | copy-start | bytes 3145732

commit v3 on v2

--- a/solution.py
+++ b/solution.py
@@ -149,6 +149,30 @@
     )(first_block, last_block, sample_ends, stacked, stacked, stacked, stacked, values, values)
 
 
+def gather_kernel(*refs):
+    *sources, out_ref = refs
+    heads = out_ref.shape[0] // len(sources)
+    for t, ref in enumerate(sources):
+        for h in range(heads):
+            out_ref[t * heads + h] = ref[:, h * HEAD_DIM:(h + 1) * HEAD_DIM]
+
+
+def by_destination_all(arrays, destinations):
+    tokens, width = arrays[0].shape[1], arrays[0].shape[2]
+    local_width = width // destinations
+    heads = local_width // HEAD_DIM
+    in_spec = pl.BlockSpec((None, tokens, local_width), lambda d: (0, 0, d))
+    return pl.pallas_call(
+        gather_kernel,
+        grid=(destinations,),
+        in_specs=[in_spec] * len(arrays),
+        out_specs=pl.BlockSpec((None, len(arrays) * heads, tokens, HEAD_DIM), lambda d: (d, 0, 0, 0)),
+        out_shape=jax.ShapeDtypeStruct(
+            (destinations, len(arrays) * heads, tokens, HEAD_DIM), arrays[0].dtype
+        ),
+    )(*arrays)
+
+
 def assemble_kernel(*refs):
     *received, out_ref, tan_ref = refs
     offset = 0
@@ -199,9 +223,7 @@
         split = array.reshape(tokens, seq_count, local_heads, HEAD_DIM)[:, :, heads]
         return jnp.transpose(split, (1, 2, 0, 3))
 
-    value_payload = jnp.concatenate(
-        [by_destination(array, slice(0, local_heads)) for array in (v_proj, v_tangent)], axis=1
-    )
+    value_payload = by_destination_all((v_proj, v_tangent), seq_count)
     values = lax.all_to_all(value_payload, "seq", split_axis=0, concat_axis=0, tiled=True)
 
     q_normed, dq_normed = normalize(q_proj, q_tangent, query_norm_gain)

time: 485 us -> 484 us (level)
  local copies, waits for them, and re-layouts: 61.3 us -> 45.4 us
  waiting for transfers between devices: 195 us -> 209 us
  Pallas kernels: 112 us -> 119 us
    all_to_all x4, waiting for transfers between devices: 106 us -> 120 us  [per_device_body(): lax.all_to_all(payload, 'seq', split_axis=0, concat_axis=0, tiled=True)]
    unnamed x56 -> x54, local copies, waits for them, and re-layouts: 47.1 us -> 39 us
    reshape x2 -> x0, local copies, waits for them, and re-layouts: 7.81 us -> none  [by_destination(): split = array.reshape(tokens, seq_count, local_heads, HEAD_DIM)[:, :, heads]]
    pallas_call x0 -> x1, Pallas kernels: none -> 6.75 us  [by_destination_all(): pl.pallas_call(gather_kernel, grid=(destinations,), in_specs=[in_spec] *...]
  transfers between devices with their start and end apart: 6 -> 6, of which waited for: 4 -> 4; matrix products, arithmetic and copies ran while one was open for 10% -> 6% of each run, Pallas kernels for 22% -> 23%
where the time goes in v3:
time: 484 us; the launch traced here: 483 us
  waiting for transfers between devices  209 us (43%)
  Pallas kernels  119 us (25%)
  blocking collectives  53.3 us (11%)
  local copies, waits for them, and re-layouts  45.4 us (9%)
  starting transfers between devices  29.5 us (6%)
  other arithmetic  25.6 us (5%)
    all_to_all x4, waiting for transfers between devices, per_device_body(): lax.all_to_all(payload, 'seq', split_axis=0, concat_axis=0, tiled=True)  120 us
    pallas_call x4, Pallas kernels, attend(): pl.pallas_call(attention_kernel, grid_spec=grid_spec, out_shape=jax.Shape...  105 us
    all_to_all x1, waiting for transfers between devices, per_device_body(): lax.all_to_all(value_payload, 'seq', split_axis=0, concat_axis=0, tiled=T...  89.4 us
    all_to_all x1, blocking collectives, per_device_body(): lax.all_to_all(group, 'seq', split_axis=0, concat_axis=0, tiled=True)  53.3 us
    unnamed x54, local copies, waits for them, and re-layouts  39 us
    all_to_all x4, starting transfers between devices, per_device_body(): lax.all_to_all(payload, 'seq', split_axis=0, concat_axis=0, tiled=True)  19.1 us
    concatenate x4, other arithmetic, per_device_body(): jnp.concatenate([by_destination(array, heads) for array in normed], axis=1)  10.2 us
  transfers between devices with their start and end apart: 6, of which 4 were waited for; matrix products, arithmetic and copies ran while one was open for 6% of the time, Pallas kernels for 23%

profile of v3, /device:TPU:0, one launch (start us, length us, event | category | flops | bytes accessed | tf_op | source)
XLA Modules:
  0.0 482.6 jit_solution(2564251653077223945)
XLA Ops:
  0.6 3.3 copy.31
  3.9 4.1 copy.33
  8.0 2.6 fusion.6
  10.7 2.4 fusion.8
  18.4 3.3 copy.35
  21.7 4.1 copy.37
  25.8 2.6 fusion.11
  28.4 2.4 fusion.13
  32.2 2.1 copy.62
  37.0 2.9 pad_maximum_fusion.3
  39.9 7.3 %all-to-all-start.4 = ((bf16[8,4,256,128]{3,2,1,0:T(8,128)(2,1)}), bf16[8,4,256,128]{3,2,1,0:T(8,128)(2,1)S(1)}, u32[]{:S(2)}, u32[]{:S(2)}) async-start(bf16[8,4,256,128]{3,2,1,0:T(8,128)(2,1)} %pad_maximum_fusion.3), calls=%async_computation.4 | async-start | bytes 4194304 | tf_op jit(solution)/shard_map/all_to_all | solution.py:238
  51.3 2.1 copy.57
  53.4 2.1 copy.58
  55.4 3.1 pad_maximum_fusion.1
  58.5 36.9 %all-to-all-done.4.q_ref.dq_ref.k_ref.dk_ref = bf16[8,4,256,128]{3,2,1,0:T(8,128)(2,1)S(1)} async-done(((bf16[8,4,256,128]{3,2,1,0:T(8,128)(2,1)}), bf16[8,4,256,128]{3,2,1,0:T(8,128)(2,1)S(1)}, u32[]{:S(2)}, u32[]{:S(2)}) %all-to-all-start.4) | async-done | bytes 2097184 | tf_op jit(solution)/shard_map/all_to_all | solution.py:238
  96.8 4.4 all-to-all-start.2
  105.3 2.6 pad_maximum_fusion.4
  107.9 41.1 %all-to-all-done.2.q_ref.dq_ref.k_ref.dk_ref = bf16[8,4,256,128]{3,2,1,0:T(8,128)(2,1)} async-done(((bf16[8,4,256,128]{3,2,1,0:T(8,128)(2,1)}), bf16[8,4,256,128]{3,2,1,0:T(8,128)(2,1)}, u32[]{:S(2)}, u32[]{:S(2)}) %all-to-all-start.2) | async-done | bytes 2097184 | tf_op jit(solution)/shard_map/all_to_all | solution.py:238
  149.0 3.6 all-to-all-start.5
  152.6 6.8 %shard_map.104 = bf16[8,8,256,128]{3,2,1,0:T(8,128)(2,1)} custom-call(bf16[1,256,4096]{2,1,0:T(8,128)(2,1)} %refs_0_.1, bf16[1,256,4096]{2,1,0:T(8,128)(2,1)} %refs_1_.1), custom_call_target="tpu_custom_call" | custom-call | tf_op jit(solution)/shard_map/pallas_call | solution.py:165
  159.4 41.7 %all-to-all-done.5.q_ref.dq_ref.k_ref.dk_ref = bf16[8,4,256,128]{3,2,1,0:T(8,128)(2,1)S(1)} async-done(((bf16[8,4,256,128]{3,2,1,0:T(8,128)(2,1)}), bf16[8,4,256,128]{3,2,1,0:T(8,128)(2,1)S(1)}, u32[]{:S(2)}, u32[]{:S(2)}) %all-to-all-start.5) | async-done | bytes 2097184 | tf_op jit(solution)/shard_map/all_to_all | solution.py:238
  202.5 4.6 all-to-all-start.1
  210.2 89.4 %all-to-all-done.1.v_ref.dv_ref = bf16[8,8,256,128]{3,2,1,0:T(8,128)(2,1)} async-done(((bf16[8,8,256,128]{3,2,1,0:T(8,128)(2,1)}), bf16[8,8,256,128]{3,2,1,0:T(8,128)(2,1)}, u32[]{:S(2)}, u32[]{:S(2)}) %all-to-all-start.1) | async-done | bytes 4194336 | tf_op jit(solution)/shard_map/all_to_all | solution.py:227
  299.6 3.8 all-to-all-start
  305.6 26.2 %shard_map.108 = bf16[8,2,256,128]{3,2,1,0:T(8,128)(2,1)} custom-call(s32[8]{0:T(128)} %get-tuple-element.10.first_ref, s32[8]{0:T(128)} %get-tuple-element.9.last_ref, s32[4]{0:T(128)} %bitcast.28, bf16[8,4,256,128]{3,2,1,0:T(8,128)(2,1)} %copy-done.2, bf16[8,4,256,128]{3,2,1,0:T(8,128)(2,1)} %copy-done.2, bf16[8,4,256,128]{3,2,1,0:T(8,128)(2,1)} %copy-done.2, ...), custom_call_target="tpu_custom_call" | custom-call | tf_op jit(solution)/shard_map/pallas_call | solution.py:142
  331.8 26.3 %shard_map.107 = bf16[8,2,256,128]{3,2,1,0:T(8,128)(2,1)} custom-call(s32[8]{0:T(128)} %get-tuple-element.10.first_ref, s32[8]{0:T(128)} %get-tuple-element.9.last_ref, s32[4]{0:T(128)} %bitcast.29, bf16[8,4,256,128]{3,2,1,0:T(8,128)(2,1)} %copy-done.1, bf16[8,4,256,128]{3,2,1,0:T(8,128)(2,1)} %copy-done.1, bf16[8,4,256,128]{3,2,1,0:T(8,128)(2,1)} %copy-done.1, ...), custom_call_target="tpu_custom_call" | custom-call | tf_op jit(solution)/shard_map/pallas_call | solution.py:142
  358.1 2.9 pad_maximum_fusion.5
  362.3 5.8 %all-to-all-start.6 = ((bf16[8,2,256,256]{3,2,1,0:T(8,128)(2,1)}), bf16[8,2,256,256]{3,2,1,0:T(8,128)(2,1)}, u32[]{:S(2)}, u32[]{:S(2)}) async-start(bf16[8,2,256,256]{3,2,1,0:T(8,128)(2,1)} %pad_maximum_fusion.5), calls=%async_computation.6 | async-start | bytes 4194304 | tf_op jit(solution)/shard_map/all_to_all | solution.py:247
  368.1 26.2 %shard_map.106 = bf16[8,2,256,128]{3,2,1,0:T(8,128)(2,1)} custom-call(s32[8]{0:T(128)} %get-tuple-element.10.first_ref, s32[8]{0:T(128)} %get-tuple-element.9.last_ref, s32[4]{0:T(128)} %bitcast.30, bf16[8,4,256,128]{3,2,1,0:T(8,128)(2,1)} %all-to-all-done.2.q_ref.dq_ref.k_ref.dk_ref, bf16[8,4,256,128]{3,2,1,0:T(8,128)(2,1)} %all-to-all-done.2.q_ref.dq_ref.k_ref.dk_ref, ...), custom_call_target="tpu_custom_call" | custom-call | tf_op jit(solution)/shard_map/pallas_call | solution.py:142
  394.3 26.3 %shard_map.105 = bf16[8,2,256,128]{3,2,1,0:T(8,128)(2,1)} custom-call(s32[8]{0:T(128)} %get-tuple-element.10.first_ref, s32[8]{0:T(128)} %get-tuple-element.9.last_ref, s32[4]{0:T(128)} %bitcast.31, bf16[8,4,256,128]{3,2,1,0:T(8,128)(2,1)} %copy-done.3, bf16[8,4,256,128]{3,2,1,0:T(8,128)(2,1)} %copy-done.3, bf16[8,4,256,128]{3,2,1,0:T(8,128)(2,1)} %copy-done.3, ...), custom_call_target="tpu_custom_call" | custom-call | tf_op jit(solution)/shard_map/pallas_call | solution.py:142
  422.2 53.3 %all_to_all.35.refs_0_ = bf16[8,2,256,256]{3,2,1,0:T(8,128)(2,1)} all-to-all(bf16[8,2,256,256]{3,2,1,0:T(8,128)(2,1)S(1)} %pad_maximum_fusion.2), channel_id=1, replica_groups=mesh['groups'=2,'seq'=8,'samp'=2] {'seq'}, dimensions={0} | all-to-all | bytes 4194304 | tf_op jit(solution)/shard_map/all_to_all | solution.py:247
  475.4 7.2 %shard_map.109 = (f32[1,256,4096]{2,1,0:T(8,128)}, f32[1,256,4096]{2,1,0:T(8,128)}) custom-call(bf16[8,2,256,256]{3,2,1,0:T(8,128)(2,1)} %all_to_all.35.refs_0_, bf16[8,2,256,256]{3,2,1,0:T(8,128)(2,1)} %all-to-all-done.6.refs_1_), custom_call_target="tpu_custom_call" | custom-call | tf_op jit(solution)/shard_map/pallas_call | solution.py:193
  (69 shorter events, 28.5 us)
Async XLA Ops:
  8.0 2.6 copy-start.4
  8.0 2.7 copy-start.14
  13.1 2.1 copy-start.6
  25.8 2.6 copy-start.5
  25.8 2.7 copy-start.15
  30.9 3.4 copy-start.7
  39.9 55.5 %all-to-all-start.4 = ((bf16[8,4,256,128]{3,2,1,0:T(8,128)(2,1)}), bf16[8,4,256,128]{3,2,1,0:T(8,128)(2,1)S(1)}, u32[]{:S(2)}, u32[]{:S(2)}) async-start(bf16[8,4,256,128]{3,2,1,0:T(8,128)(2,1)} %pad_maximum_fusion.3), calls=%async_computation.4 | async-start | bytes 4194304 | tf_op jit(solution)/shard_map/all_to_all | solution.py:238
  95.5 1.4 copy-start.1
  96.8 52.2 %all-to-all-start.2 = ((bf16[8,4,256,128]{3,2,1,0:T(8,128)(2,1)}), bf16[8,4,256,128]{3,2,1,0:T(8,128)(2,1)}, u32[]{:S(2)}, u32[]{:S(2)}) async-start(bf16[8,4,256,128]{3,2,1,0:T(8,128)(2,1)} %pad_maximum_fusion.1), calls=%async_computation.2 | async-start | bytes 4194304 | tf_op jit(solution)/shard_map/all_to_all | solution.py:238
  101.2 2.7 copy-start.13
  101.2 3.8 copy-start.12
  149.0 52.0 %all-to-all-start.5 = ((bf16[8,4,256,128]{3,2,1,0:T(8,128)(2,1)}), bf16[8,4,256,128]{3,2,1,0:T(8,128)(2,1)S(1)}, u32[]{:S(2)}, u32[]{:S(2)}) async-start(bf16[8,4,256,128]{3,2,1,0:T(8,128)(2,1)} %pad_maximum_fusion.4), calls=%async_computation.5 | async-start | bytes 4194304 | tf_op jit(solution)/shard_map/all_to_all | solution.py:238
  201.1 1.4 copy-start.2
  202.5 97.1 %all-to-all-start.1 = ((bf16[8,8,256,128]{3,2,1,0:T(8,128)(2,1)}), bf16[8,8,256,128]{3,2,1,0:T(8,128)(2,1)}, u32[]{:S(2)}, u32[]{:S(2)}) async-start(bf16[8,8,256,128]{3,2,1,0:T(8,128)(2,1)} %shard_map.104), calls=%async_computation.1 | async-start | bytes 8388608 | tf_op jit(solution)/shard_map/all_to_all | solution.py:227
  207.0 1.0 copy-start.11
  207.0 1.3 copy-start.10
  210.2 93.2 %copy-start.16 = (s32[2,4]{1,0:T(2,128)S(1)}, s32[2,4]{1,0:T(2,128)}, u32[]{:S(2)}) copy-start(s32[2,4]{1,0:T(2,128)} %param.19) | copy-start | bytes 100
  299.6 61.4 %all-to-all-start = ((bf16[8,4,256,128]{3,2,1,0:T(8,128)(2,1)}), bf16[8,4,256,128]{3,2,1,0:T(8,128)(2,1)S(1)}, u32[]{:S(2)}, u32[]{:S(2)}) async-start(bf16[8,4,256,128]{3,2,1,0:T(8,128)(2,1)} %pad_maximum_fusion), calls=%async_computation | async-start | bytes 4194304 | tf_op jit(solution)/shard_map/all_to_all | solution.py:238
  303.6 2.0 copy-start
  331.8 26.3 %copy-start.9 = (bf16[8,2,256,128]{3,2,1,0:T(8,128)(2,1)S(1)}, bf16[8,2,256,128]{3,2,1,0:T(8,128)(2,1)}, u32[]{:S(2)}) copy-start(bf16[8,2,256,128]{3,2,1,0:T(8,128)(2,1)} %shard_map.108) | copy-start | bytes 3145732
  361.0 1.3 copy-start.3
  362.3 59.9 %all-to-all-start.6 = ((bf16[8,2,256,256]{3,2,1,0:T(8,128)(2,1)}), bf16[8,2,256,256]{3,2,1,0:T(8,128)(2,1)}, u32[]{:S(2)}, u32[]{:S(2)}) async-start(bf16[8,2,256,256]{3,2,1,0:T(8,128)(2,1)} %pad_maximum_fusion.5), calls=%async_computation.6 | async-start | bytes 4194304 | tf_op jit(solution)/shard_map/all_to_all | solution.py:247
  394.3 26.3 %copy-start.8 = (bf16[8,2,256,128]{3,2,1,0:T(8,128)(2,1)S(1)}, bf16[8,2,256,128]{3,2,1,0:T(8,128)(2,1)}, u32[]{:S(2)}) copy-start(bf16[8,2,256,128]{3,2,1,0:T(8,128)(2,1)} %shard_map.106) | copy-start | bytes 3145732

commit v4 on v3

--- a/solution.py
+++ b/solution.py
@@ -173,23 +173,22 @@
     )(*arrays)
 
 
-def assemble_kernel(*refs):
-    *received, out_ref, tan_ref = refs
-    offset = 0
-    for r in received:
-        w = r.shape[-1]
-        out_ref[:, offset:offset + w] = r[0].astype(jnp.float32)
-        tan_ref[:, offset:offset + w] = r[1].astype(jnp.float32)
-        offset += w
-
-
-def assemble(received, tokens, width):
-    sources = received[0].shape[0]
-    local_width = width // sources
-    in_specs = [
-        pl.BlockSpec((None, 2, tokens, r.shape[3]), lambda s: (s, 0, 0, 0)) for r in received
-    ]
-    out_spec = pl.BlockSpec((None, tokens, local_width), lambda s: (0, 0, s))
+def assemble_kernel(received_ref, *refs):
+    out_ref, tan_ref = refs[-2], refs[-1]
+    out_ref[...] = received_ref[0].astype(jnp.float32)
+    tan_ref[...] = received_ref[1].astype(jnp.float32)
+
+
+def assemble_part(received, part, parts, previous, tokens, width):
+    sources, _, _, part_width = received.shape
+    in_specs = [pl.BlockSpec((None, 2, tokens, part_width), lambda s: (s, 0, 0, 0))]
+    out_spec = pl.BlockSpec((None, tokens, part_width), lambda s: (0, 0, s * parts + part))
+    operands = [received]
+    aliases = {}
+    if previous is not None:
+        in_specs += [pl.BlockSpec(memory_space=pl.ANY), pl.BlockSpec(memory_space=pl.ANY)]
+        operands += list(previous)
+        aliases = {1: 0, 2: 1}
     return pl.pallas_call(
         assemble_kernel,
         grid=(sources,),
@@ -199,7 +198,8 @@
             jax.ShapeDtypeStruct((1, tokens, width), jnp.float32),
             jax.ShapeDtypeStruct((1, tokens, width), jnp.float32),
         ],
-    )(*received)
+        input_output_aliases=aliases,
+    )(*operands)
 
 
 CHUNKS = 4
@@ -241,11 +241,13 @@
             first_block, last_block, sample_ends, RESULT_DTYPE,
         )
         results.append(result)
-    received = []
-    for g in range(0, chunks, 2):
-        group = jnp.concatenate(results[g:g + 2], axis=3)
-        received.append(lax.all_to_all(group, "seq", split_axis=0, concat_axis=0, tiled=True))
-    return tuple(assemble(received, tokens, width))
+    groups = [results[g:g + 2] for g in range(0, chunks, 2)]
+    outputs = None
+    for g, members in enumerate(groups):
+        group = jnp.concatenate(members, axis=3)
+        received = lax.all_to_all(group, "seq", split_axis=0, concat_axis=0, tiled=True)
+        outputs = assemble_part(received, g, len(groups), outputs, tokens, width)
+    return tuple(outputs)
 
 
 def solution(mesh):

time: 484 us -> 486 us (level)
  blocking collectives: 53.3 us -> 0 us
  waiting for transfers between devices: 209 us -> 250 us
  starting transfers between devices: 29.5 us -> 35.5 us
  Pallas kernels: 119 us -> 124 us
    all_to_all x1 -> x0, blocking collectives: 53.3 us -> none  [per_device_body(): lax.all_to_all(group, 'seq', split_axis=0, concat_axis=0, tiled=True)]
    all_to_all x1 -> x2, waiting for transfers between devices: 0.01 us -> 41.3 us  [per_device_body(): lax.all_to_all(group, 'seq', split_axis=0, concat_axis=0, tiled=True)]
    all_to_all x1 -> x2, starting transfers between devices: 5.82 us -> 11.8 us  [per_device_body(): lax.all_to_all(group, 'seq', split_axis=0, concat_axis=0, tiled=True)]
    pallas_call x1 -> x2, Pallas kernels: 7.17 us -> 11.9 us  [assemble_part(): pl.pallas_call(assemble_kernel, grid=(sources,), in_specs=in_specs, out_s...]
    unnamed x54 -> x56, local copies, waits for them, and re-layouts: 39 us -> 40.4 us
  transfers between devices with their start and end apart: 6 -> 7, of which waited for: 4 -> 5; matrix products, arithmetic and copies ran while one was open for 6% -> 6% of each run, Pallas kernels for 23% -> 24%
where the time goes in v4:
time: 486 us; the launch traced here: 484 us
  waiting for transfers between devices  250 us (51%)
  Pallas kernels  124 us (26%)
  local copies, waits for them, and re-layouts  46.7 us (10%)
  starting transfers between devices  35.5 us (7%)
  other arithmetic  27 us (6%)
    all_to_all x4, waiting for transfers between devices, per_device_body(): lax.all_to_all(payload, 'seq', split_axis=0, concat_axis=0, tiled=True)  120 us
    pallas_call x4, Pallas kernels, attend(): pl.pallas_call(attention_kernel, grid_spec=grid_spec, out_shape=jax.Shape...  105 us
    all_to_all x1, waiting for transfers between devices, per_device_body(): lax.all_to_all(value_payload, 'seq', split_axis=0, concat_axis=0, tiled=T...  89.4 us
    all_to_all x2, waiting for transfers between devices, per_device_body(): lax.all_to_all(group, 'seq', split_axis=0, concat_axis=0, tiled=True)  41.3 us
    unnamed x56, local copies, waits for them, and re-layouts  40.4 us
    all_to_all x4, starting transfers between devices, per_device_body(): lax.all_to_all(payload, 'seq', split_axis=0, concat_axis=0, tiled=True)  19.1 us
    pallas_call x2, Pallas kernels, assemble_part(): pl.pallas_call(assemble_kernel, grid=(sources,), in_specs=in_specs, out_s...  11.9 us
    all_to_all x2, starting transfers between devices, per_device_body(): lax.all_to_all(group, 'seq', split_axis=0, concat_axis=0, tiled=True)  11.8 us
  transfers between devices with their start and end apart: 7, of which 5 were waited for; matrix products, arithmetic and copies ran while one was open for 6% of the time, Pallas kernels for 24%

profile of v4, /device:TPU:0, one launch (start us, length us, event | category | flops | bytes accessed | tf_op | source)
XLA Modules:
  0.0 484.2 jit_solution(1529547275730340793)
XLA Ops:
  0.6 3.3 copy.33
  3.9 4.1 copy.35
  8.0 2.6 fusion.6
  10.7 2.4 fusion.8
  18.4 3.3 copy.37
  21.7 4.1 copy.39
  25.8 2.6 fusion.11
  28.5 2.4 fusion.13
  37.0 2.9 pad_maximum_fusion.3
  39.9 7.3 %all-to-all-start.4 = ((bf16[8,4,256,128]{3,2,1,0:T(8,128)(2,1)}), bf16[8,4,256,128]{3,2,1,0:T(8,128)(2,1)S(1)}, u32[]{:S(2)}, u32[]{:S(2)}) async-start(bf16[8,4,256,128]{3,2,1,0:T(8,128)(2,1)} %pad_maximum_fusion.3), calls=%async_computation.4 | async-start | bytes 4194304 | tf_op jit(solution)/shard_map/all_to_all | solution.py:238
  55.4 3.1 pad_maximum_fusion.1
  58.5 37.0 %all-to-all-done.4.q_ref.dq_ref.k_ref.dk_ref = bf16[8,4,256,128]{3,2,1,0:T(8,128)(2,1)S(1)} async-done(((bf16[8,4,256,128]{3,2,1,0:T(8,128)(2,1)}), bf16[8,4,256,128]{3,2,1,0:T(8,128)(2,1)S(1)}, u32[]{:S(2)}, u32[]{:S(2)}) %all-to-all-start.4) | async-done | bytes 2097184 | tf_op jit(solution)/shard_map/all_to_all | solution.py:238
  96.9 4.4 all-to-all-start.2
  105.3 2.6 pad_maximum_fusion.4
  108.0 41.1 %all-to-all-done.2.q_ref.dq_ref.k_ref.dk_ref = bf16[8,4,256,128]{3,2,1,0:T(8,128)(2,1)} async-done(((bf16[8,4,256,128]{3,2,1,0:T(8,128)(2,1)}), bf16[8,4,256,128]{3,2,1,0:T(8,128)(2,1)}, u32[]{:S(2)}, u32[]{:S(2)}) %all-to-all-start.2) | async-done | bytes 2097184 | tf_op jit(solution)/shard_map/all_to_all | solution.py:238
  149.0 3.6 all-to-all-start.5
  152.7 6.8 %shard_map.104 = bf16[8,8,256,128]{3,2,1,0:T(8,128)(2,1)} custom-call(bf16[1,256,4096]{2,1,0:T(8,128)(2,1)} %refs_0_.1, bf16[1,256,4096]{2,1,0:T(8,128)(2,1)} %refs_1_.1), custom_call_target="tpu_custom_call" | custom-call | tf_op jit(solution)/shard_map/pallas_call | solution.py:165
  159.4 41.7 %all-to-all-done.5.q_ref.dq_ref.k_ref.dk_ref = bf16[8,4,256,128]{3,2,1,0:T(8,128)(2,1)S(1)} async-done(((bf16[8,4,256,128]{3,2,1,0:T(8,128)(2,1)}), bf16[8,4,256,128]{3,2,1,0:T(8,128)(2,1)S(1)}, u32[]{:S(2)}, u32[]{:S(2)}) %all-to-all-start.5) | async-done | bytes 2097184 | tf_op jit(solution)/shard_map/all_to_all | solution.py:238
  202.5 4.6 all-to-all-start.1
  210.2 89.4 %all-to-all-done.1.v_ref.dv_ref = bf16[8,8,256,128]{3,2,1,0:T(8,128)(2,1)} async-done(((bf16[8,8,256,128]{3,2,1,0:T(8,128)(2,1)}), bf16[8,8,256,128]{3,2,1,0:T(8,128)(2,1)}, u32[]{:S(2)}, u32[]{:S(2)}) %all-to-all-start.1) | async-done | bytes 4194336 | tf_op jit(solution)/shard_map/all_to_all | solution.py:227
  299.6 3.8 all-to-all-start
  305.7 26.2 %shard_map.108 = bf16[8,2,256,128]{3,2,1,0:T(8,128)(2,1)} custom-call(s32[8]{0:T(128)} %get-tuple-element.14.first_ref, s32[8]{0:T(128)} %get-tuple-element.13.last_ref, s32[4]{0:T(128)} %bitcast.28, bf16[8,4,256,128]{3,2,1,0:T(8,128)(2,1)} %copy-done.2, bf16[8,4,256,128]{3,2,1,0:T(8,128)(2,1)} %copy-done.2, bf16[8,4,256,128]{3,2,1,0:T(8,128)(2,1)} %copy-done.2, ...), custom_call_target="tpu_custom_call" | custom-call | tf_op jit(solution)/shard_map/pallas_call | solution.py:142
  331.8 26.3 %shard_map.107 = bf16[8,2,256,128]{3,2,1,0:T(8,128)(2,1)} custom-call(s32[8]{0:T(128)} %get-tuple-element.14.first_ref, s32[8]{0:T(128)} %get-tuple-element.13.last_ref, s32[4]{0:T(128)} %bitcast.29, bf16[8,4,256,128]{3,2,1,0:T(8,128)(2,1)} %copy-done.1, bf16[8,4,256,128]{3,2,1,0:T(8,128)(2,1)} %copy-done.1, bf16[8,4,256,128]{3,2,1,0:T(8,128)(2,1)} %copy-done.1, ...), custom_call_target="tpu_custom_call" | custom-call | tf_op jit(solution)/shard_map/pallas_call | solution.py:142
  358.2 2.9 pad_maximum_fusion.5
  362.4 5.8 %all-to-all-start.6 = ((bf16[8,2,256,256]{3,2,1,0:T(8,128)(2,1)}), bf16[8,2,256,256]{3,2,1,0:T(8,128)(2,1)}, u32[]{:S(2)}, u32[]{:S(2)}) async-start(bf16[8,2,256,256]{3,2,1,0:T(8,128)(2,1)} %pad_maximum_fusion.5), calls=%async_computation.6 | async-start | bytes 4194304 | tf_op jit(solution)/shard_map/all_to_all | solution.py:248
  368.2 26.2 %shard_map.106 = bf16[8,2,256,128]{3,2,1,0:T(8,128)(2,1)} custom-call(s32[8]{0:T(128)} %get-tuple-element.14.first_ref, s32[8]{0:T(128)} %get-tuple-element.13.last_ref, s32[4]{0:T(128)} %bitcast.30, bf16[8,4,256,128]{3,2,1,0:T(8,128)(2,1)} %all-to-all-done.2.q_ref.dq_ref.k_ref.dk_ref, bf16[8,4,256,128]{3,2,1,0:T(8,128)(2,1)} %all-to-all-done.2.q_ref.dq_ref.k_ref.dk_ref, ...), custom_call_target="tpu_custom_call" | custom-call | tf_op jit(solution)/shard_map/pallas_call | solution.py:142
  394.4 26.3 %shard_map.105 = bf16[8,2,256,128]{3,2,1,0:T(8,128)(2,1)} custom-call(s32[8]{0:T(128)} %get-tuple-element.14.first_ref, s32[8]{0:T(128)} %get-tuple-element.13.last_ref, s32[4]{0:T(128)} %bitcast.31, bf16[8,4,256,128]{3,2,1,0:T(8,128)(2,1)} %copy-done.3, bf16[8,4,256,128]{3,2,1,0:T(8,128)(2,1)} %copy-done.3, bf16[8,4,256,128]{3,2,1,0:T(8,128)(2,1)} %copy-done.3, ...), custom_call_target="tpu_custom_call" | custom-call | tf_op jit(solution)/shard_map/pallas_call | solution.py:142
  420.8 2.8 pad_maximum_fusion.2
  423.6 6.0 %all-to-all-start.3 = ((bf16[8,2,256,256]{3,2,1,0:T(8,128)(2,1)}), bf16[8,2,256,256]{3,2,1,0:T(8,128)(2,1)S(1)}, u32[]{:S(2)}, u32[]{:S(2)}) async-start(bf16[8,2,256,256]{3,2,1,0:T(8,128)(2,1)} %pad_maximum_fusion.2), calls=%async_computation.3 | async-start | bytes 4194304 | tf_op jit(solution)/shard_map/all_to_all | solution.py:248
  429.6 6.0 %shard_map.109 = (f32[1,256,4096]{2,1,0:T(8,128)}, f32[1,256,4096]{2,1,0:T(8,128)}) custom-call(bf16[8,2,256,256]{3,2,1,0:T(8,128)(2,1)} %all-to-all-done.6.received_ref), custom_call_target="tpu_custom_call" | custom-call | tf_op jit(solution)/shard_map/pallas_call | solution.py:192
  435.6 41.3 %all-to-all-done.3.received_ref = bf16[8,2,256,256]{3,2,1,0:T(8,128)(2,1)S(1)} async-done(((bf16[8,2,256,256]{3,2,1,0:T(8,128)(2,1)}), bf16[8,2,256,256]{3,2,1,0:T(8,128)(2,1)S(1)}, u32[]{:S(2)}, u32[]{:S(2)}) %all-to-all-start.3) | async-done | bytes 2097184 | tf_op jit(solution)/shard_map/all_to_all | solution.py:248
  478.2 5.9 %shard_map.110 = (f32[1,256,4096]{2,1,0:T(8,128)}, f32[1,256,4096]{2,1,0:T(8,128)}) custom-call(bf16[8,2,256,256]{3,2,1,0:T(8,128)(2,1)} %copy-done.8, f32[1,256,4096]{2,1,0:T(8,128)} %get-tuple-element.5.refs_0_, f32[1,256,4096]{2,1,0:T(8,128)} %get-tuple-element.6.refs_1_), custom_call_target="tpu_custom_call", output_to_operand_aliasing={{0}: (1, {}), {1}: (2, {})} | custom-call | tf_op jit(solution)/shard_map/pallas_call | solution.py:192
  (73 shorter events, 34.6 us)
Async XLA Ops:
  8.0 2.6 copy-start.4
  8.0 2.7 copy-start.15
  13.1 2.2 copy-start.6
  25.8 2.6 copy-start.5
  25.8 2.7 copy-start.16
  30.9 3.4 copy-start.7
  39.9 55.5 %all-to-all-start.4 = ((bf16[8,4,256,128]{3,2,1,0:T(8,128)(2,1)}), bf16[8,4,256,128]{3,2,1,0:T(8,128)(2,1)S(1)}, u32[]{:S(2)}, u32[]{:S(2)}) async-start(bf16[8,4,256,128]{3,2,1,0:T(8,128)(2,1)} %pad_maximum_fusion.3), calls=%async_computation.4 | async-start | bytes 4194304 | tf_op jit(solution)/shard_map/all_to_all | solution.py:238
  95.5 1.4 copy-start.1
  96.9 52.2 %all-to-all-start.2 = ((bf16[8,4,256,128]{3,2,1,0:T(8,128)(2,1)}), bf16[8,4,256,128]{3,2,1,0:T(8,128)(2,1)}, u32[]{:S(2)}, u32[]{:S(2)}) async-start(bf16[8,4,256,128]{3,2,1,0:T(8,128)(2,1)} %pad_maximum_fusion.1), calls=%async_computation.2 | async-start | bytes 4194304 | tf_op jit(solution)/shard_map/all_to_all | solution.py:238
  101.2 2.7 copy-start.14
  101.2 3.8 copy-start.13
  149.0 52.0 %all-to-all-start.5 = ((bf16[8,4,256,128]{3,2,1,0:T(8,128)(2,1)}), bf16[8,4,256,128]{3,2,1,0:T(8,128)(2,1)S(1)}, u32[]{:S(2)}, u32[]{:S(2)}) async-start(bf16[8,4,256,128]{3,2,1,0:T(8,128)(2,1)} %pad_maximum_fusion.4), calls=%async_computation.5 | async-start | bytes 4194304 | tf_op jit(solution)/shard_map/all_to_all | solution.py:238
  201.1 1.4 copy-start.2
  202.5 97.1 %all-to-all-start.1 = ((bf16[8,8,256,128]{3,2,1,0:T(8,128)(2,1)}), bf16[8,8,256,128]{3,2,1,0:T(8,128)(2,1)}, u32[]{:S(2)}, u32[]{:S(2)}) async-start(bf16[8,8,256,128]{3,2,1,0:T(8,128)(2,1)} %shard_map.104), calls=%async_computation.1 | async-start | bytes 8388608 | tf_op jit(solution)/shard_map/all_to_all | solution.py:227
  207.1 1.0 copy-start.12
  207.1 1.3 copy-start.11
  210.2 93.2 %copy-start.17 = (s32[2,4]{1,0:T(2,128)S(1)}, s32[2,4]{1,0:T(2,128)}, u32[]{:S(2)}) copy-start(s32[2,4]{1,0:T(2,128)} %param.19) | copy-start | bytes 100
  299.6 61.5 %all-to-all-start = ((bf16[8,4,256,128]{3,2,1,0:T(8,128)(2,1)}), bf16[8,4,256,128]{3,2,1,0:T(8,128)(2,1)S(1)}, u32[]{:S(2)}, u32[]{:S(2)}) async-start(bf16[8,4,256,128]{3,2,1,0:T(8,128)(2,1)} %pad_maximum_fusion), calls=%async_computation | async-start | bytes 4194304 | tf_op jit(solution)/shard_map/all_to_all | solution.py:238
  303.6 2.0 copy-start
  331.8 26.3 %copy-start.10 = (bf16[8,2,256,128]{3,2,1,0:T(8,128)(2,1)S(1)}, bf16[8,2,256,128]{3,2,1,0:T(8,128)(2,1)}, u32[]{:S(2)}) copy-start(bf16[8,2,256,128]{3,2,1,0:T(8,128)(2,1)} %shard_map.108) | copy-start | bytes 3145732
  361.1 1.3 copy-start.3
  362.4 61.2 %all-to-all-start.6 = ((bf16[8,2,256,256]{3,2,1,0:T(8,128)(2,1)}), bf16[8,2,256,256]{3,2,1,0:T(8,128)(2,1)}, u32[]{:S(2)}, u32[]{:S(2)}) async-start(bf16[8,2,256,256]{3,2,1,0:T(8,128)(2,1)} %pad_maximum_fusion.5), calls=%async_computation.6 | async-start | bytes 4194304 | tf_op jit(solution)/shard_map/all_to_all | solution.py:248
  394.4 26.3 %copy-start.9 = (bf16[8,2,256,128]{3,2,1,0:T(8,128)(2,1)S(1)}, bf16[8,2,256,128]{3,2,1,0:T(8,128)(2,1)}, u32[]{:S(2)}) copy-start(bf16[8,2,256,128]{3,2,1,0:T(8,128)(2,1)} %shard_map.106) | copy-start | bytes 3145732
  423.6 53.3 %all-to-all-start.3 = ((bf16[8,2,256,256]{3,2,1,0:T(8,128)(2,1)}), bf16[8,2,256,256]{3,2,1,0:T(8,128)(2,1)S(1)}, u32[]{:S(2)}, u32[]{:S(2)}) async-start(bf16[8,2,256,256]{3,2,1,0:T(8,128)(2,1)} %pad_maximum_fusion.2), calls=%async_computation.3 | async-start | bytes 4194304 | tf_op jit(solution)/shard_map/all_to_all | solution.py:248
  476.9 1.3 copy-start.8

commit v5 on v4

--- a/solution.py
+++ b/solution.py
@@ -1,3 +1,4 @@
+import functools
 import math
 
 import jax
@@ -151,52 +152,79 @@
 
 def gather_kernel(*refs):
     *sources, out_ref = refs
-    heads = out_ref.shape[0] // len(sources)
-    for t, ref in enumerate(sources):
-        for h in range(heads):
-            out_ref[t * heads + h] = ref[:, h * HEAD_DIM:(h + 1) * HEAD_DIM]
+    per_step = out_ref.shape[0]
+    heads = out_ref.shape[1] // len(sources)
+    for d in range(per_step):
+        for t, ref in enumerate(sources):
+            for h in range(heads):
+                column = (d * heads + h) * HEAD_DIM
+                out_ref[d, t * heads + h] = ref[:, column:column + HEAD_DIM]
+
+
+GATHER_STEPS = 2
 
 
 def by_destination_all(arrays, destinations):
     tokens, width = arrays[0].shape[1], arrays[0].shape[2]
     local_width = width // destinations
     heads = local_width // HEAD_DIM
-    in_spec = pl.BlockSpec((None, tokens, local_width), lambda d: (0, 0, d))
+    steps = GATHER_STEPS if destinations % GATHER_STEPS == 0 else 1
+    per_step = destinations // steps
+    in_spec = pl.BlockSpec((None, tokens, per_step * local_width), lambda d: (0, 0, d))
     return pl.pallas_call(
         gather_kernel,
-        grid=(destinations,),
+        grid=(steps,),
         in_specs=[in_spec] * len(arrays),
-        out_specs=pl.BlockSpec((None, len(arrays) * heads, tokens, HEAD_DIM), lambda d: (d, 0, 0, 0)),
+        out_specs=pl.BlockSpec(
+            (per_step, len(arrays) * heads, tokens, HEAD_DIM), lambda d: (d, 0, 0, 0)
+        ),
         out_shape=jax.ShapeDtypeStruct(
             (destinations, len(arrays) * heads, tokens, HEAD_DIM), arrays[0].dtype
         ),
     )(*arrays)
 
 
-def assemble_kernel(received_ref, *refs):
-    out_ref, tan_ref = refs[-2], refs[-1]
-    out_ref[...] = received_ref[0].astype(jnp.float32)
-    tan_ref[...] = received_ref[1].astype(jnp.float32)
+def assemble_kernel(part, parts, received_ref, *refs):
+    out_ref, tan_ref, staged, widened, load_sem, store_sems = refs[-6:]
+    sources, _, _, part_width = staged.shape
+    local_width = part_width * parts
+    load = pltpu.make_async_copy(received_ref, staged, load_sem)
+    load.start()
+    load.wait()
+    stores = []
+    for s in range(sources):
+        column = s * local_width + part * part_width
+        for p, target in enumerate((out_ref, tan_ref)):
+            widened[p, s] = staged[s, p].astype(jnp.float32)
+            store = pltpu.make_async_copy(
+                widened.at[p, s], target.at[0, :, pl.ds(column, part_width)], store_sems.at[p, s]
+            )
+            store.start()
+            stores.append(store)
+    for store in stores:
+        store.wait()
 
 
 def assemble_part(received, part, parts, previous, tokens, width):
     sources, _, _, part_width = received.shape
-    in_specs = [pl.BlockSpec((None, 2, tokens, part_width), lambda s: (s, 0, 0, 0))]
-    out_spec = pl.BlockSpec((None, tokens, part_width), lambda s: (0, 0, s * parts + part))
     operands = [received]
     aliases = {}
     if previous is not None:
-        in_specs += [pl.BlockSpec(memory_space=pl.ANY), pl.BlockSpec(memory_space=pl.ANY)]
         operands += list(previous)
         aliases = {1: 0, 2: 1}
     return pl.pallas_call(
-        assemble_kernel,
-        grid=(sources,),
-        in_specs=in_specs,
-        out_specs=[out_spec, out_spec],
+        functools.partial(assemble_kernel, part, parts),
+        in_specs=[pl.BlockSpec(memory_space=pl.ANY)] * len(operands),
+        out_specs=[pl.BlockSpec(memory_space=pl.ANY), pl.BlockSpec(memory_space=pl.ANY)],
         out_shape=[
             jax.ShapeDtypeStruct((1, tokens, width), jnp.float32),
             jax.ShapeDtypeStruct((1, tokens, width), jnp.float32),
+        ],
+        scratch_shapes=[
+            pltpu.VMEM((sources, 2, tokens, part_width), received.dtype),
+            pltpu.VMEM((2, sources, tokens, part_width), jnp.float32),
+            pltpu.SemaphoreType.DMA(()),
+            pltpu.SemaphoreType.DMA((2, sources)),
         ],
         input_output_aliases=aliases,
     )(*operands)
@@ -241,7 +269,7 @@
             first_block, last_block, sample_ends, RESULT_DTYPE,
         )
         results.append(result)
-    groups = [results[g:g + 2] for g in range(0, chunks, 2)]
+    groups = [results[g:g + 2] for g in range(0, len(results), 2)]
     outputs = None
     for g, members in enumerate(groups):
         group = jnp.concatenate(members, axis=3)

time: 486 us -> 484 us (level)
  Pallas kernels: 124 us -> 116 us
  waiting for transfers between devices: 250 us -> 255 us
    pallas_call x3, Pallas kernels: 18.7 us -> 11.4 us  [the longest x2 7.49 us: assemble_part(): pl.pallas_call(functools.partial(assemble_kernel, part, parts), in_specs=...]
  transfers between devices with their start and end apart: 7 -> 7, of which waited for: 5 -> 5; matrix products, arithmetic and copies ran while one was open for 6% -> 6% of each run, Pallas kernels for 24% -> 23%
where the time goes in v5:
time: 484 us; the launch traced here: 482 us
  waiting for transfers between devices  255 us (53%)
  Pallas kernels  116 us (24%)
  local copies, waits for them, and re-layouts  46.7 us (10%)
  starting transfers between devices  35.5 us (7%)
  other arithmetic  27 us (6%)
    all_to_all x4, waiting for transfers between devices, per_device_body(): lax.all_to_all(payload, 'seq', split_axis=0, concat_axis=0, tiled=True)  123 us
    pallas_call x4, Pallas kernels, attend(): pl.pallas_call(attention_kernel, grid_spec=grid_spec, out_shape=jax.Shape...  105 us
    all_to_all x1, waiting for transfers between devices, per_device_body(): lax.all_to_all(value_payload, 'seq', split_axis=0, concat_axis=0, tiled=T...  89.4 us
    all_to_all x2, waiting for transfers between devices, per_device_body(): lax.all_to_all(group, 'seq', split_axis=0, concat_axis=0, tiled=True)  43.5 us
    unnamed x56, local copies, waits for them, and re-layouts  40.4 us
    all_to_all x4, starting transfers between devices, per_device_body(): lax.all_to_all(payload, 'seq', split_axis=0, concat_axis=0, tiled=True)  19.1 us
    all_to_all x2, starting transfers between devices, per_device_body(): lax.all_to_all(group, 'seq', split_axis=0, concat_axis=0, tiled=True)  11.8 us
    concatenate x4, other arithmetic, per_device_body(): jnp.concatenate([by_destination(array, heads) for array in normed], axis=1)  10.2 us
  transfers between devices with their start and end apart: 7, of which 5 were waited for; matrix products, arithmetic and copies ran while one was open for 6% of the time, Pallas kernels for 23%

profile of v5, /device:TPU:0, one launch (start us, length us, event | category | flops | bytes accessed | tf_op | source)
XLA Modules:
  0.0 482.1 jit_solution(11200886970875430831)
XLA Ops:
  0.6 3.3 copy.33
  3.9 4.1 copy.35
  8.0 2.6 fusion.6
  10.7 2.4 fusion.8
  18.4 3.3 copy.37
  21.7 4.1 copy.39
  25.8 2.6 fusion.11
  28.5 2.4 fusion.13
  37.0 2.9 pad_maximum_fusion.3
  39.9 7.3 %all-to-all-start.4 = ((bf16[8,4,256,128]{3,2,1,0:T(8,128)(2,1)}), bf16[8,4,256,128]{3,2,1,0:T(8,128)(2,1)S(1)}, u32[]{:S(2)}, u32[]{:S(2)}) async-start(bf16[8,4,256,128]{3,2,1,0:T(8,128)(2,1)} %pad_maximum_fusion.3), calls=%async_computation.4 | async-start | bytes 4194304 | tf_op jit(solution)/shard_map/all_to_all | solution.py:266
  55.4 3.1 pad_maximum_fusion.1
  58.5 37.0 %all-to-all-done.4.q_ref.dq_ref.k_ref.dk_ref = bf16[8,4,256,128]{3,2,1,0:T(8,128)(2,1)S(1)} async-done(((bf16[8,4,256,128]{3,2,1,0:T(8,128)(2,1)}), bf16[8,4,256,128]{3,2,1,0:T(8,128)(2,1)S(1)}, u32[]{:S(2)}, u32[]{:S(2)}) %all-to-all-start.4) | async-done | bytes 2097184 | tf_op jit(solution)/shard_map/all_to_all | solution.py:266
  96.9 4.4 all-to-all-start.2
  105.3 2.6 pad_maximum_fusion.4
  108.0 41.1 %all-to-all-done.2.q_ref.dq_ref.k_ref.dk_ref = bf16[8,4,256,128]{3,2,1,0:T(8,128)(2,1)} async-done(((bf16[8,4,256,128]{3,2,1,0:T(8,128)(2,1)}), bf16[8,4,256,128]{3,2,1,0:T(8,128)(2,1)}, u32[]{:S(2)}, u32[]{:S(2)}) %all-to-all-start.2) | async-done | bytes 2097184 | tf_op jit(solution)/shard_map/all_to_all | solution.py:266
  149.0 3.6 all-to-all-start.5
  152.7 3.9 shard_map.104
  156.6 44.5 %all-to-all-done.5.q_ref.dq_ref.k_ref.dk_ref = bf16[8,4,256,128]{3,2,1,0:T(8,128)(2,1)S(1)} async-done(((bf16[8,4,256,128]{3,2,1,0:T(8,128)(2,1)}), bf16[8,4,256,128]{3,2,1,0:T(8,128)(2,1)S(1)}, u32[]{:S(2)}, u32[]{:S(2)}) %all-to-all-start.5) | async-done | bytes 2097184 | tf_op jit(solution)/shard_map/all_to_all | solution.py:266
  202.5 4.6 all-to-all-start.1
  210.2 89.4 %all-to-all-done.1.v_ref.dv_ref = bf16[8,8,256,128]{3,2,1,0:T(8,128)(2,1)} async-done(((bf16[8,8,256,128]{3,2,1,0:T(8,128)(2,1)}), bf16[8,8,256,128]{3,2,1,0:T(8,128)(2,1)}, u32[]{:S(2)}, u32[]{:S(2)}) %all-to-all-start.1) | async-done | bytes 4194336 | tf_op jit(solution)/shard_map/all_to_all | solution.py:255
  299.6 3.8 all-to-all-start
  305.7 26.2 %shard_map.108 = bf16[8,2,256,128]{3,2,1,0:T(8,128)(2,1)} custom-call(s32[8]{0:T(128)} %get-tuple-element.14.first_ref, s32[8]{0:T(128)} %get-tuple-element.13.last_ref, s32[4]{0:T(128)} %bitcast.28, bf16[8,4,256,128]{3,2,1,0:T(8,128)(2,1)} %copy-done.2, bf16[8,4,256,128]{3,2,1,0:T(8,128)(2,1)} %copy-done.2, bf16[8,4,256,128]{3,2,1,0:T(8,128)(2,1)} %copy-done.2, ...), custom_call_target="tpu_custom_call" | custom-call | tf_op jit(solution)/shard_map/pallas_call | solution.py:143
  331.8 26.3 %shard_map.107 = bf16[8,2,256,128]{3,2,1,0:T(8,128)(2,1)} custom-call(s32[8]{0:T(128)} %get-tuple-element.14.first_ref, s32[8]{0:T(128)} %get-tuple-element.13.last_ref, s32[4]{0:T(128)} %bitcast.29, bf16[8,4,256,128]{3,2,1,0:T(8,128)(2,1)} %copy-done.1, bf16[8,4,256,128]{3,2,1,0:T(8,128)(2,1)} %copy-done.1, bf16[8,4,256,128]{3,2,1,0:T(8,128)(2,1)} %copy-done.1, ...), custom_call_target="tpu_custom_call" | custom-call | tf_op jit(solution)/shard_map/pallas_call | solution.py:143
  358.2 2.9 pad_maximum_fusion.5
  362.4 5.8 %all-to-all-start.6 = ((bf16[8,2,256,256]{3,2,1,0:T(8,128)(2,1)}), bf16[8,2,256,256]{3,2,1,0:T(8,128)(2,1)}, u32[]{:S(2)}, u32[]{:S(2)}) async-start(bf16[8,2,256,256]{3,2,1,0:T(8,128)(2,1)} %pad_maximum_fusion.5), calls=%async_computation.6 | async-start | bytes 4194304 | tf_op jit(solution)/shard_map/all_to_all | solution.py:276
  368.2 26.2 %shard_map.106 = bf16[8,2,256,128]{3,2,1,0:T(8,128)(2,1)} custom-call(s32[8]{0:T(128)} %get-tuple-element.14.first_ref, s32[8]{0:T(128)} %get-tuple-element.13.last_ref, s32[4]{0:T(128)} %bitcast.30, bf16[8,4,256,128]{3,2,1,0:T(8,128)(2,1)} %all-to-all-done.2.q_ref.dq_ref.k_ref.dk_ref, bf16[8,4,256,128]{3,2,1,0:T(8,128)(2,1)} %all-to-all-done.2.q_ref.dq_ref.k_ref.dk_ref, ...), custom_call_target="tpu_custom_call" | custom-call | tf_op jit(solution)/shard_map/pallas_call | solution.py:143
  394.4 26.3 %shard_map.105 = bf16[8,2,256,128]{3,2,1,0:T(8,128)(2,1)} custom-call(s32[8]{0:T(128)} %get-tuple-element.14.first_ref, s32[8]{0:T(128)} %get-tuple-element.13.last_ref, s32[4]{0:T(128)} %bitcast.31, bf16[8,4,256,128]{3,2,1,0:T(8,128)(2,1)} %copy-done.3, bf16[8,4,256,128]{3,2,1,0:T(8,128)(2,1)} %copy-done.3, bf16[8,4,256,128]{3,2,1,0:T(8,128)(2,1)} %copy-done.3, ...), custom_call_target="tpu_custom_call" | custom-call | tf_op jit(solution)/shard_map/pallas_call | solution.py:143
  420.8 2.8 pad_maximum_fusion.2
  423.6 6.0 %all-to-all-start.3 = ((bf16[8,2,256,256]{3,2,1,0:T(8,128)(2,1)}), bf16[8,2,256,256]{3,2,1,0:T(8,128)(2,1)S(1)}, u32[]{:S(2)}, u32[]{:S(2)}) async-start(bf16[8,2,256,256]{3,2,1,0:T(8,128)(2,1)} %pad_maximum_fusion.2), calls=%async_computation.3 | async-start | bytes 4194304 | tf_op jit(solution)/shard_map/all_to_all | solution.py:276
  429.6 3.7 shard_map.109
  433.4 43.5 %all-to-all-done.3.received_ref = bf16[8,2,256,256]{3,2,1,0:T(8,128)(2,1)S(1)} async-done(((bf16[8,2,256,256]{3,2,1,0:T(8,128)(2,1)}), bf16[8,2,256,256]{3,2,1,0:T(8,128)(2,1)S(1)}, u32[]{:S(2)}, u32[]{:S(2)}) %all-to-all-start.3) | async-done | bytes 2097184 | tf_op jit(solution)/shard_map/all_to_all | solution.py:276
  478.2 3.7 shard_map.110
  (73 shorter events, 34.6 us)
Async XLA Ops:
  8.0 2.6 copy-start.4
  8.0 2.7 copy-start.15
  13.1 2.2 copy-start.6
  25.8 2.6 copy-start.5
  25.8 2.7 copy-start.16
  30.9 3.4 copy-start.7
  39.9 55.5 %all-to-all-start.4 = ((bf16[8,4,256,128]{3,2,1,0:T(8,128)(2,1)}), bf16[8,4,256,128]{3,2,1,0:T(8,128)(2,1)S(1)}, u32[]{:S(2)}, u32[]{:S(2)}) async-start(bf16[8,4,256,128]{3,2,1,0:T(8,128)(2,1)} %pad_maximum_fusion.3), calls=%async_computation.4 | async-start | bytes 4194304 | tf_op jit(solution)/shard_map/all_to_all | solution.py:266
  95.5 1.4 copy-start.1
  96.9 52.2 %all-to-all-start.2 = ((bf16[8,4,256,128]{3,2,1,0:T(8,128)(2,1)}), bf16[8,4,256,128]{3,2,1,0:T(8,128)(2,1)}, u32[]{:S(2)}, u32[]{:S(2)}) async-start(bf16[8,4,256,128]{3,2,1,0:T(8,128)(2,1)} %pad_maximum_fusion.1), calls=%async_computation.2 | async-start | bytes 4194304 | tf_op jit(solution)/shard_map/all_to_all | solution.py:266
  101.2 2.7 copy-start.14
  101.2 3.8 copy-start.13
  149.0 52.0 %all-to-all-start.5 = ((bf16[8,4,256,128]{3,2,1,0:T(8,128)(2,1)}), bf16[8,4,256,128]{3,2,1,0:T(8,128)(2,1)S(1)}, u32[]{:S(2)}, u32[]{:S(2)}) async-start(bf16[8,4,256,128]{3,2,1,0:T(8,128)(2,1)} %pad_maximum_fusion.4), calls=%async_computation.5 | async-start | bytes 4194304 | tf_op jit(solution)/shard_map/all_to_all | solution.py:266
  201.1 1.4 copy-start.2
  202.5 97.1 %all-to-all-start.1 = ((bf16[8,8,256,128]{3,2,1,0:T(8,128)(2,1)}), bf16[8,8,256,128]{3,2,1,0:T(8,128)(2,1)}, u32[]{:S(2)}, u32[]{:S(2)}) async-start(bf16[8,8,256,128]{3,2,1,0:T(8,128)(2,1)} %shard_map.104), calls=%async_computation.1 | async-start | bytes 8388608 | tf_op jit(solution)/shard_map/all_to_all | solution.py:255
  207.1 1.0 copy-start.12
  207.1 1.3 copy-start.11
  210.2 93.2 %copy-start.17 = (s32[2,4]{1,0:T(2,128)S(1)}, s32[2,4]{1,0:T(2,128)}, u32[]{:S(2)}) copy-start(s32[2,4]{1,0:T(2,128)} %param.19) | copy-start | bytes 100
  299.6 61.5 %all-to-all-start = ((bf16[8,4,256,128]{3,2,1,0:T(8,128)(2,1)}), bf16[8,4,256,128]{3,2,1,0:T(8,128)(2,1)S(1)}, u32[]{:S(2)}, u32[]{:S(2)}) async-start(bf16[8,4,256,128]{3,2,1,0:T(8,128)(2,1)} %pad_maximum_fusion), calls=%async_computation | async-start | bytes 4194304 | tf_op jit(solution)/shard_map/all_to_all | solution.py:266
  303.6 2.0 copy-start
  331.8 26.3 %copy-start.10 = (bf16[8,2,256,128]{3,2,1,0:T(8,128)(2,1)S(1)}, bf16[8,2,256,128]{3,2,1,0:T(8,128)(2,1)}, u32[]{:S(2)}) copy-start(bf16[8,2,256,128]{3,2,1,0:T(8,128)(2,1)} %shard_map.108) | copy-start | bytes 3145732
  361.1 1.3 copy-start.3
  362.4 61.2 %all-to-all-start.6 = ((bf16[8,2,256,256]{3,2,1,0:T(8,128)(2,1)}), bf16[8,2,256,256]{3,2,1,0:T(8,128)(2,1)}, u32[]{:S(2)}, u32[]{:S(2)}) async-start(bf16[8,2,256,256]{3,2,1,0:T(8,128)(2,1)} %pad_maximum_fusion.5), calls=%async_computation.6 | async-start | bytes 4194304 | tf_op jit(solution)/shard_map/all_to_all | solution.py:276
  394.4 26.3 %copy-start.9 = (bf16[8,2,256,128]{3,2,1,0:T(8,128)(2,1)S(1)}, bf16[8,2,256,128]{3,2,1,0:T(8,128)(2,1)}, u32[]{:S(2)}) copy-start(bf16[8,2,256,128]{3,2,1,0:T(8,128)(2,1)} %shard_map.106) | copy-start | bytes 3145732
  423.6 53.3 %all-to-all-start.3 = ((bf16[8,2,256,256]{3,2,1,0:T(8,128)(2,1)}), bf16[8,2,256,256]{3,2,1,0:T(8,128)(2,1)S(1)}, u32[]{:S(2)}, u32[]{:S(2)}) async-start(bf16[8,2,256,256]{3,2,1,0:T(8,128)(2,1)} %pad_maximum_fusion.2), calls=%async_computation.3 | async-start | bytes 4194304 | tf_op jit(solution)/shard_map/all_to_all | solution.py:276
  476.9 1.3 copy-start.8

commit v6 on v2

--- a/solution.py
+++ b/solution.py
@@ -151,24 +151,32 @@
 
 def assemble_kernel(*refs):
     *received, out_ref, tan_ref = refs
-    offset = 0
-    for r in received:
-        w = r.shape[-1]
-        out_ref[:, offset:offset + w] = r[0].astype(jnp.float32)
-        tan_ref[:, offset:offset + w] = r[1].astype(jnp.float32)
-        offset += w
+    per_step = received[0].shape[0]
+    local_width = out_ref.shape[1] // per_step
+    for s in range(per_step):
+        offset = s * local_width
+        for r in received:
+            w = r.shape[-1]
+            out_ref[:, offset:offset + w] = r[s, 0].astype(jnp.float32)
+            tan_ref[:, offset:offset + w] = r[s, 1].astype(jnp.float32)
+            offset += w
+
+
+ASSEMBLE_STEPS = 2
 
 
 def assemble(received, tokens, width):
     sources = received[0].shape[0]
     local_width = width // sources
+    steps = ASSEMBLE_STEPS if sources % ASSEMBLE_STEPS == 0 else 1
+    per_step = sources // steps
     in_specs = [
-        pl.BlockSpec((None, 2, tokens, r.shape[3]), lambda s: (s, 0, 0, 0)) for r in received
+        pl.BlockSpec((per_step, 2, tokens, r.shape[3]), lambda s: (s, 0, 0, 0)) for r in received
     ]
-    out_spec = pl.BlockSpec((None, tokens, local_width), lambda s: (0, 0, s))
+    out_spec = pl.BlockSpec((None, tokens, per_step * local_width), lambda s: (0, 0, s))
     return pl.pallas_call(
         assemble_kernel,
-        grid=(sources,),
+        grid=(steps,),
         in_specs=in_specs,
         out_specs=[out_spec, out_spec],
         out_shape=[
@@ -199,10 +207,23 @@
         split = array.reshape(tokens, seq_count, local_heads, HEAD_DIM)[:, :, heads]
         return jnp.transpose(split, (1, 2, 0, 3))
 
-    value_payload = jnp.concatenate(
-        [by_destination(array, slice(0, local_heads)) for array in (v_proj, v_tangent)], axis=1
-    )
-    values = lax.all_to_all(value_payload, "seq", split_axis=0, concat_axis=0, tiled=True)
+    me = lax.axis_index("seq")
+    local_width = local_heads * HEAD_DIM
+    both = jnp.stack(
+        [array.reshape(tokens, seq_count, local_width) for array in (v_proj, v_tangent)], axis=0
+    )
+    pieces = [lax.dynamic_index_in_dim(both, me, 2, keepdims=False)]
+    for d in range(1, seq_count):
+        piece = lax.dynamic_index_in_dim(both, (me + d) % seq_count, 2, keepdims=False)
+        pieces.append(lax.ppermute(
+            piece, "seq", [(s, (s + d) % seq_count) for s in range(seq_count)]
+        ))
+    by_shift = jnp.stack(pieces, axis=0)
+    order = (me - jnp.arange(seq_count, dtype=jnp.int32)) % seq_count
+    by_source = jnp.take(by_shift, order, axis=0)
+    values = jnp.transpose(
+        by_source.reshape(seq_count, 2, tokens, local_heads, HEAD_DIM), (0, 1, 3, 2, 4)
+    ).reshape(seq_count, 2 * local_heads, tokens, HEAD_DIM)
 
     q_normed, dq_normed = normalize(q_proj, q_tangent, query_norm_gain)
     k_normed, dk_normed = normalize(k_proj, k_tangent, key_norm_gain)

time: 485 us -> 521 us (1.074)
  starting transfers between devices: 29.7 us -> 67.9 us
  waiting for transfers between devices: 195 us -> 159 us
  local copies, waits for them, and re-layouts: 61.3 us -> 88.4 us
  other arithmetic: 30.2 us -> 39.2 us
    all_to_all x1 -> x0, waiting for transfers between devices: 89.2 us -> none  [per_device_body(): lax.all_to_all(value_payload, 'seq', split_axis=0, concat_axis=0, tiled=T...]
    ppermute x0 -> x7, waiting for transfers between devices: none -> 34.9 us  [per_device_body(): lax.ppermute(piece, 'seq', [(s, (s + d) % seq_count) for s in range(seq_c...]
    all_to_all x1, starting transfers between devices: 5.99 us -> 33.4 us  [per_device_body(): lax.all_to_all(group, 'seq', split_axis=0, concat_axis=0, tiled=True)]
    all_to_all x4, waiting for transfers between devices: 106 us -> 124 us  [per_device_body(): lax.all_to_all(payload, 'seq', split_axis=0, concat_axis=0, tiled=True)]
    ppermute x0 -> x7, starting transfers between devices: none -> 14.8 us  [per_device_body(): lax.ppermute(piece, 'seq', [(s, (s + d) % seq_count) for s in range(seq_c...]
    unnamed x56 -> x57, local copies, waits for them, and re-layouts: 47.1 us -> 61.5 us
    dynamic_slice x0 -> x8, local copies, waits for them, and re-layouts: none -> 13.6 us  [the longest x7 12.6 us: per_device_body(): lax.dynamic_index_in_dim(both, (me + d) % seq_count, 2, keepdims=False)]
    reshape x2 -> x0, local copies, waits for them, and re-layouts: 7.81 us -> none  [by_destination(): split = array.reshape(tokens, seq_count, local_heads, HEAD_DIM)[:, :, heads]]
  transfers between devices with their start and end apart: 6 -> 12, of which waited for: 4 -> 6; matrix products, arithmetic and copies ran while one was open for 10% -> 17% of each run, Pallas kernels for 22% -> 20%
where the time goes in v6:
time: 521 us; the launch traced here: 519 us
  waiting for transfers between devices  159 us (31%)
  Pallas kernels  110 us (21%)
  local copies, waits for them, and re-layouts  88.4 us (17%)
  starting transfers between devices  67.9 us (13%)
  blocking collectives  53 us (10%)
  other arithmetic  39.2 us (8%)
    all_to_all x4, waiting for transfers between devices, per_device_body(): lax.all_to_all(payload, 'seq', split_axis=0, concat_axis=0, tiled=True)  124 us
    pallas_call x4, Pallas kernels, attend(): pl.pallas_call(attention_kernel, grid_spec=grid_spec, out_shape=jax.Shape...  105 us
    unnamed x57, local copies, waits for them, and re-layouts  61.5 us
    all_to_all x1, blocking collectives, per_device_body(): lax.all_to_all(group, 'seq', split_axis=0, concat_axis=0, tiled=True)  53 us
    ppermute x7, waiting for transfers between devices, per_device_body(): lax.ppermute(piece, 'seq', [(s, (s + d) % seq_count) for s in range(seq_c...  34.9 us
    all_to_all x1, starting transfers between devices, per_device_body(): lax.all_to_all(group, 'seq', split_axis=0, concat_axis=0, tiled=True)  33.4 us
    all_to_all x4, starting transfers between devices, per_device_body(): lax.all_to_all(payload, 'seq', split_axis=0, concat_axis=0, tiled=True)  19.6 us
    ppermute x7, starting transfers between devices, per_device_body(): lax.ppermute(piece, 'seq', [(s, (s + d) % seq_count) for s in range(seq_c...  14.8 us
  transfers between devices with their start and end apart: 12, of which 6 were waited for; matrix products, arithmetic and copies ran while one was open for 17% of the time, Pallas kernels for 20%

profile of v6, /device:TPU:0, one launch (start us, length us, event | category | flops | bytes accessed | tf_op | source)
XLA Modules:
  0.0 518.9 jit_solution(12113934400739289355)
XLA Ops:
  0.6 3.3 copy.61
  3.9 4.1 copy.63
  8.0 2.6 fusion.6
  18.4 3.3 copy.65
  21.7 4.1 copy.67
  37.0 2.9 pad_maximum_fusion.4
  39.9 7.3 %all-to-all-start.3 = ((bf16[8,4,256,128]{3,2,1,0:T(8,128)(2,1)}), bf16[8,4,256,128]{3,2,1,0:T(8,128)(2,1)S(1)}, u32[]{:S(2)}, u32[]{:S(2)}) async-start(bf16[8,4,256,128]{3,2,1,0:T(8,128)(2,1)} %pad_maximum_fusion.4), calls=%async_computation.3 | async-start | bytes 4194304 | tf_op jit(solution)/shard_map/all_to_all | solution.py:237
  55.5 3.1 pad_maximum_fusion.5
  58.6 36.9 %all-to-all-done.3.q_ref.dq_ref.k_ref.dk_ref = bf16[8,4,256,128]{3,2,1,0:T(8,128)(2,1)S(1)} async-done(((bf16[8,4,256,128]{3,2,1,0:T(8,128)(2,1)}), bf16[8,4,256,128]{3,2,1,0:T(8,128)(2,1)S(1)}, u32[]{:S(2)}, u32[]{:S(2)}) %all-to-all-start.3) | async-done | bytes 2097184 | tf_op jit(solution)/shard_map/all_to_all | solution.py:237
  95.5 4.4 all-to-all-start.4
  104.6 2.8 pad_maximum_fusion.1
  107.4 40.3 %all-to-all-done.4.q_ref.dq_ref.k_ref.dk_ref = bf16[8,4,256,128]{3,2,1,0:T(8,128)(2,1)} async-done(((bf16[8,4,256,128]{3,2,1,0:T(8,128)(2,1)}), bf16[8,4,256,128]{3,2,1,0:T(8,128)(2,1)}, u32[]{:S(2)}, u32[]{:S(2)}) %all-to-all-start.4) | async-done | bytes 2097184 | tf_op jit(solution)/shard_map/all_to_all | solution.py:237
  147.7 3.6 all-to-all-start
  151.3 4.1 copy.69
  155.4 4.1 copy.70
  159.5 3.3 fusion.16
  194.7 3.2 pad_maximum_fusion.2
  198.7 47.1 %all-to-all-done.q_ref.dq_ref.k_ref.dk_ref = bf16[8,4,256,128]{3,2,1,0:T(8,128)(2,1)S(1)} async-done(((bf16[8,4,256,128]{3,2,1,0:T(8,128)(2,1)}), bf16[8,4,256,128]{3,2,1,0:T(8,128)(2,1)S(1)}, u32[]{:S(2)}, u32[]{:S(2)}) %all-to-all-start) | async-done | bytes 2097184 | tf_op jit(solution)/shard_map/all_to_all | solution.py:237
  245.8 4.4 all-to-all-start.1
  254.5 3.8 collective-permute-start.5
  271.1 31.0 %collective-permute-done.5 = bf16[2,256,512]{2,1,0:T(8,128)(2,1)S(1)} collective-permute-done((bf16[2,256,512]{2,1,0:T(8,128)(2,1)}, bf16[2,256,512]{2,1,0:T(8,128)(2,1)S(1)}, u32[]{:S(2)}, u32[]{:S(2)}) %collective-permute-start.5) | collective-permute-done | bytes 524320 | tf_op jit(solution)/shard_map/ppermute | solution.py:218
  305.5 5.0 gather_fusion
  310.6 2.7 broadcast_select_fusion
  316.5 26.2 %shard_map.106 = bf16[8,2,256,128]{3,2,1,0:T(8,128)(2,1)} custom-call(s32[8]{0:T(128)} %get-tuple-element.10.first_ref, s32[8]{0:T(128)} %get-tuple-element.9.last_ref, s32[4]{0:T(128)} %bitcast.56, bf16[8,4,256,128]{3,2,1,0:T(8,128)(2,1)} %copy-done.1, bf16[8,4,256,128]{3,2,1,0:T(8,128)(2,1)} %copy-done.1, bf16[8,4,256,128]{3,2,1,0:T(8,128)(2,1)} %copy-done.1, ...), custom_call_target="tpu_custom_call" | custom-call | tf_op jit(solution)/shard_map/pallas_call | solution.py:142
  342.7 26.3 %shard_map.107 = bf16[8,2,256,128]{3,2,1,0:T(8,128)(2,1)} custom-call(s32[8]{0:T(128)} %get-tuple-element.10.first_ref, s32[8]{0:T(128)} %get-tuple-element.9.last_ref, s32[4]{0:T(128)} %bitcast.57, bf16[8,4,256,128]{3,2,1,0:T(8,128)(2,1)} %all-to-all-done.4.q_ref.dq_ref.k_ref.dk_ref, bf16[8,4,256,128]{3,2,1,0:T(8,128)(2,1)} %all-to-all-done.4.q_ref.dq_ref.k_ref.dk_ref, ...), custom_call_target="tpu_custom_call" | custom-call | tf_op jit(solution)/shard_map/pallas_call | solution.py:142
  369.1 2.8 pad_maximum_fusion.6
  371.9 33.4 %all-to-all-start.5 = ((bf16[8,2,256,256]{3,2,1,0:T(8,128)(2,1)}), bf16[8,2,256,256]{3,2,1,0:T(8,128)(2,1)S(1)}, u32[]{:S(2)}, u32[]{:S(2)}) async-start(bf16[8,2,256,256]{3,2,1,0:T(8,128)(2,1)} %pad_maximum_fusion.6), calls=%async_computation.5 | async-start | bytes 4194304 | tf_op jit(solution)/shard_map/all_to_all | solution.py:246
  405.3 26.2 %shard_map.104 = bf16[8,2,256,128]{3,2,1,0:T(8,128)(2,1)} custom-call(s32[8]{0:T(128)} %get-tuple-element.10.first_ref, s32[8]{0:T(128)} %get-tuple-element.9.last_ref, s32[4]{0:T(128)} %bitcast.58, bf16[8,4,256,128]{3,2,1,0:T(8,128)(2,1)} %copy-done.2, bf16[8,4,256,128]{3,2,1,0:T(8,128)(2,1)} %copy-done.2, bf16[8,4,256,128]{3,2,1,0:T(8,128)(2,1)} %copy-done.2, ...), custom_call_target="tpu_custom_call" | custom-call | tf_op jit(solution)/shard_map/pallas_call | solution.py:142
  431.5 26.3 %shard_map.105 = bf16[8,2,256,128]{3,2,1,0:T(8,128)(2,1)} custom-call(s32[8]{0:T(128)} %get-tuple-element.10.first_ref, s32[8]{0:T(128)} %get-tuple-element.9.last_ref, s32[4]{0:T(128)} %bitcast.59, bf16[8,4,256,128]{3,2,1,0:T(8,128)(2,1)} %all-to-all-done.1.q_ref.dq_ref.k_ref.dk_ref, bf16[8,4,256,128]{3,2,1,0:T(8,128)(2,1)} %all-to-all-done.1.q_ref.dq_ref.k_ref.dk_ref, ...), custom_call_target="tpu_custom_call" | custom-call | tf_op jit(solution)/shard_map/pallas_call | solution.py:142
  457.9 2.8 pad_maximum_fusion.3
  460.7 53.0 %all_to_all.30.refs_0_ = bf16[8,2,256,256]{3,2,1,0:T(8,128)(2,1)} all-to-all(bf16[8,2,256,256]{3,2,1,0:T(8,128)(2,1)} %pad_maximum_fusion.3), channel_id=1, replica_groups=mesh['groups'=2,'seq'=8,'samp'=2] {'seq'}, dimensions={0} | all-to-all | bytes 4194304 | tf_op jit(solution)/shard_map/all_to_all | solution.py:246
  513.8 5.1 shard_map.108
  (101 shorter events, 88.4 us)
Async XLA Ops:
  3.9 6.7 %copy-start.11 = (f32[4096]{0:T(1024)S(1)}, f32[4096]{0:T(1024)}, u32[]{:S(2)}) copy-start(f32[4096]{0:T(1024)} %param.17) | copy-start | bytes 49156
  8.0 2.7 copy-start.3
  13.1 2.1 copy-start.5
  21.7 6.7 %copy-start.12 = (f32[4096]{0:T(1024)S(1)}, f32[4096]{0:T(1024)}, u32[]{:S(2)}) copy-start(f32[4096]{0:T(1024)} %param.18) | copy-start | bytes 49156
  25.8 2.7 copy-start.4
  30.9 3.4 copy-start.6
  39.9 55.5 %all-to-all-start.3 = ((bf16[8,4,256,128]{3,2,1,0:T(8,128)(2,1)}), bf16[8,4,256,128]{3,2,1,0:T(8,128)(2,1)S(1)}, u32[]{:S(2)}, u32[]{:S(2)}) async-start(bf16[8,4,256,128]{3,2,1,0:T(8,128)(2,1)} %pad_maximum_fusion.4), calls=%async_computation.3 | async-start | bytes 4194304 | tf_op jit(solution)/shard_map/all_to_all | solution.py:237
  95.5 9.1 %copy-start.1 = (bf16[8,4,256,128]{3,2,1,0:T(8,128)(2,1)}, bf16[8,4,256,128]{3,2,1,0:T(8,128)(2,1)S(1)}, u32[]{:S(2)}) copy-start(bf16[8,4,256,128]{3,2,1,0:T(8,128)(2,1)S(1)} %all-to-all-done.3.q_ref.dq_ref.k_ref.dk_ref) | copy-start | bytes 6291460
  95.5 52.2 %all-to-all-start.4 = ((bf16[8,4,256,128]{3,2,1,0:T(8,128)(2,1)}), bf16[8,4,256,128]{3,2,1,0:T(8,128)(2,1)}, u32[]{:S(2)}, u32[]{:S(2)}) async-start(bf16[8,4,256,128]{3,2,1,0:T(8,128)(2,1)} %pad_maximum_fusion.5), calls=%async_computation.4 | async-start | bytes 4194304 | tf_op jit(solution)/shard_map/all_to_all | solution.py:237
  147.7 98.2 %all-to-all-start = ((bf16[8,4,256,128]{3,2,1,0:T(8,128)(2,1)}), bf16[8,4,256,128]{3,2,1,0:T(8,128)(2,1)S(1)}, u32[]{:S(2)}, u32[]{:S(2)}) async-start(bf16[8,4,256,128]{3,2,1,0:T(8,128)(2,1)} %pad_maximum_fusion.1), calls=%async_computation | async-start | bytes 4194304 | tf_op jit(solution)/shard_map/all_to_all | solution.py:237
  164.9 89.5 %collective-permute-start = (bf16[2,256,512]{2,1,0:T(8,128)(2,1)}, bf16[2,256,512]{2,1,0:T(8,128)(2,1)}, u32[]{:S(2)}, u32[]{:S(2)}) collective-permute-start(bf16[2,256,512]{2,1,0:T(8,128)(2,1)} %bitcast.95), channel_id=1, source_target_pairs={{0,2},{2,4},{4,6},{6,8},{8,10},{10,12},{12,14},{14,0},{1,3},{3,5},... | collective-permute-start | bytes 1572872 | tf_op jit(solution)/shard_map/ppermute | solution.py:218
  168.9 91.2 %collective-permute-start.1 = (bf16[2,256,512]{2,1,0:T(8,128)(2,1)}, bf16[2,256,512]{2,1,0:T(8,128)(2,1)}, u32[]{:S(2)}, u32[]{:S(2)}) collective-permute-start(bf16[2,256,512]{2,1,0:T(8,128)(2,1)} %bitcast.94), channel_id=1, source_target_pairs={{0,4},{2,6},{4,8},{6,10},{8,12},{10,14},{12,0},{14,2},{1,5},{3,7},... | collective-permute-start | bytes 1572872 | tf_op jit(solution)/shard_map/ppermute | solution.py:218
  172.5 93.1 %collective-permute-start.2 = (bf16[2,256,512]{2,1,0:T(8,128)(2,1)}, bf16[2,256,512]{2,1,0:T(8,128)(2,1)}, u32[]{:S(2)}, u32[]{:S(2)}) collective-permute-start(bf16[2,256,512]{2,1,0:T(8,128)(2,1)} %bitcast.93), channel_id=1, source_target_pairs={{0,6},{2,8},{4,10},{6,12},{8,14},{10,0},{12,2},{14,4},{1,7},{3,9},... | collective-permute-start | bytes 1572872 | tf_op jit(solution)/shard_map/ppermute | solution.py:218
  174.8 11.3 %copy-start.13 = (s32[2,4]{1,0:T(2,128)S(1)}, s32[2,4]{1,0:T(2,128)}, u32[]{:S(2)}) copy-start(s32[2,4]{1,0:T(2,128)} %param.19) | copy-start | bytes 100
  176.9 90.5 %collective-permute-start.3 = (bf16[2,256,512]{2,1,0:T(8,128)(2,1)}, bf16[2,256,512]{2,1,0:T(8,128)(2,1)}, u32[]{:S(2)}, u32[]{:S(2)}) collective-permute-start(bf16[2,256,512]{2,1,0:T(8,128)(2,1)} %bitcast.92), channel_id=1, source_target_pairs={{0,8},{2,10},{4,12},{6,14},{8,0},{10,2},{12,4},{14,6},{1,9},{3,11}... | collective-permute-start | bytes 1572872 | tf_op jit(solution)/shard_map/ppermute | solution.py:218
  182.7 86.6 %collective-permute-start.4 = (bf16[2,256,512]{2,1,0:T(8,128)(2,1)}, bf16[2,256,512]{2,1,0:T(8,128)(2,1)}, u32[]{:S(2)}, u32[]{:S(2)}) collective-permute-start(bf16[2,256,512]{2,1,0:T(8,128)(2,1)} %bitcast.96), channel_id=1, source_target_pairs={{0,10},{2,12},{4,14},{6,0},{8,2},{10,4},{12,6},{14,8},{1,11},{3,13... | collective-permute-start | bytes 1572872 | tf_op jit(solution)/shard_map/ppermute | solution.py:218
  186.3 63.9 %copy-start = (s32[4,1]{0,1:T(1,128)}, s32[4,1]{0,1:T(1,128)S(1)}, u32[]{:S(2)}) copy-start(s32[4,1]{0,1:T(1,128)S(1)} %reduce-window.8) | copy-start | bytes 52
  186.3 11.5 %copy-start.10 = (bf16[2,256,1,512]{3,1,0,2:T(8,128)(2,1)S(1)}, bf16[2,256,1,512]{3,1,0,2:T(8,128)(2,1)}, u32[]{:S(2)}) copy-start(bf16[2,256,1,512]{3,1,0,2:T(8,128)(2,1)} %copy.71) | copy-start | bytes 1572868
  245.8 14.3 %copy-start.2 = (bf16[8,4,256,128]{3,2,1,0:T(8,128)(2,1)}, bf16[8,4,256,128]{3,2,1,0:T(8,128)(2,1)S(1)}, u32[]{:S(2)}) copy-start(bf16[8,4,256,128]{3,2,1,0:T(8,128)(2,1)S(1)} %all-to-all-done.q_ref.dq_ref.k_ref.dk_ref) | copy-start | bytes 6291460
  245.8 126.1 %all-to-all-start.1 = ((bf16[8,4,256,128]{3,2,1,0:T(8,128)(2,1)}), bf16[8,4,256,128]{3,2,1,0:T(8,128)(2,1)}, u32[]{:S(2)}, u32[]{:S(2)}) async-start(bf16[8,4,256,128]{3,2,1,0:T(8,128)(2,1)} %pad_maximum_fusion.2), calls=%async_computation.1 | async-start | bytes 4194304 | tf_op jit(solution)/shard_map/all_to_all | solution.py:237
  254.5 47.7 %collective-permute-start.5 = (bf16[2,256,512]{2,1,0:T(8,128)(2,1)}, bf16[2,256,512]{2,1,0:T(8,128)(2,1)S(1)}, u32[]{:S(2)}, u32[]{:S(2)}) collective-permute-start(bf16[2,256,512]{2,1,0:T(8,128)(2,1)} %bitcast.98), channel_id=1, source_target_pairs={{0,12},{2,14},{4,0},{6,2},{8,4},{10,6},{12,8},{14,10},{1,13},{3,15... | collective-permute-start | bytes 1572872 | tf_op jit(solution)/shard_map/ppermute | solution.py:218
  260.1 44.6 %collective-permute-start.6 = (bf16[2,256,512]{2,1,0:T(8,128)(2,1)S(1)}, bf16[2,256,512]{2,1,0:T(8,128)(2,1)S(1)}, u32[]{:S(2)}, u32[]{:S(2)}) collective-permute-start(bf16[2,256,512]{2,1,0:T(8,128)(2,1)S(1)} %bitcast.97), channel_id=1, source_target_pairs={{0,14},{2,0},{4,2},{6,4},{8,6},{10,8},{12,10},{14,12},{1,15},{3,1}... | collective-permute-start | bytes 1572872 | tf_op jit(solution)/shard_map/ppermute | solution.py:218
  342.7 26.3 %copy-start.9 = (bf16[8,2,256,128]{3,2,1,0:T(8,128)(2,1)S(1)}, bf16[8,2,256,128]{3,2,1,0:T(8,128)(2,1)}, u32[]{:S(2)}) copy-start(bf16[8,2,256,128]{3,2,1,0:T(8,128)(2,1)} %shard_map.106) | copy-start | bytes 3145732
  371.9 88.8 %all-to-all-start.5 = ((bf16[8,2,256,256]{3,2,1,0:T(8,128)(2,1)}), bf16[8,2,256,256]{3,2,1,0:T(8,128)(2,1)S(1)}, u32[]{:S(2)}, u32[]{:S(2)}) async-start(bf16[8,2,256,256]{3,2,1,0:T(8,128)(2,1)} %pad_maximum_fusion.6), calls=%async_computation.5 | async-start | bytes 4194304 | tf_op jit(solution)/shard_map/all_to_all | solution.py:246
  431.5 26.3 %copy-start.8 = (bf16[8,2,256,128]{3,2,1,0:T(8,128)(2,1)S(1)}, bf16[8,2,256,128]{3,2,1,0:T(8,128)(2,1)}, u32[]{:S(2)}) copy-start(bf16[8,2,256,128]{3,2,1,0:T(8,128)(2,1)} %shard_map.104) | copy-start | bytes 3145732
  460.7 53.0 %copy-start.7 = (bf16[8,2,256,256]{3,2,1,0:T(8,128)(2,1)}, bf16[8,2,256,256]{3,2,1,0:T(8,128)(2,1)S(1)}, u32[]{:S(2)}) copy-start(bf16[8,2,256,256]{3,2,1,0:T(8,128)(2,1)S(1)} %all-to-all-done.5.refs_1_) | copy-start | bytes 6291460

commit v7 on v5

--- a/solution.py
+++ b/solution.py
@@ -184,16 +184,15 @@
     )(*arrays)
 
 
-def assemble_kernel(part, parts, received_ref, *refs):
+def assemble_kernel(offset, local_width, received_ref, *refs):
     out_ref, tan_ref, staged, widened, load_sem, store_sems = refs[-6:]
     sources, _, _, part_width = staged.shape
-    local_width = part_width * parts
     load = pltpu.make_async_copy(received_ref, staged, load_sem)
     load.start()
     load.wait()
     stores = []
     for s in range(sources):
-        column = s * local_width + part * part_width
+        column = s * local_width + offset
         for p, target in enumerate((out_ref, tan_ref)):
             widened[p, s] = staged[s, p].astype(jnp.float32)
             store = pltpu.make_async_copy(
@@ -205,7 +204,7 @@
         store.wait()
 
 
-def assemble_part(received, part, parts, previous, tokens, width):
+def assemble_part(received, offset, previous, tokens, width):
     sources, _, _, part_width = received.shape
     operands = [received]
     aliases = {}
@@ -213,7 +212,7 @@
         operands += list(previous)
         aliases = {1: 0, 2: 1}
     return pl.pallas_call(
-        functools.partial(assemble_kernel, part, parts),
+        functools.partial(assemble_kernel, offset, width // sources),
         in_specs=[pl.BlockSpec(memory_space=pl.ANY)] * len(operands),
         out_specs=[pl.BlockSpec(memory_space=pl.ANY), pl.BlockSpec(memory_space=pl.ANY)],
         out_shape=[
@@ -269,12 +268,15 @@
             first_block, last_block, sample_ends, RESULT_DTYPE,
         )
         results.append(result)
-    groups = [results[g:g + 2] for g in range(0, len(results), 2)]
+    split = max(1, len(results) - 1)
+    groups = [members for members in (results[:split], results[split:]) if members]
     outputs = None
-    for g, members in enumerate(groups):
+    offset = 0
+    for members in groups:
         group = jnp.concatenate(members, axis=3)
         received = lax.all_to_all(group, "seq", split_axis=0, concat_axis=0, tiled=True)
-        outputs = assemble_part(received, g, len(groups), outputs, tokens, width)
+        outputs = assemble_part(received, offset, outputs, tokens, width)
+        offset += group.shape[3]
     return tuple(outputs)
 
 

time: 484 us -> 501 us (1.035)
  waiting for transfers between devices: 255 us -> 277 us
    all_to_all x2, waiting for transfers between devices: 43.5 us -> 65.5 us  [per_device_body(): lax.all_to_all(group, 'seq', split_axis=0, concat_axis=0, tiled=True)]
    unnamed x56 -> x54, local copies, waits for them, and re-layouts: 40.4 us -> 40 us
  transfers between devices with their start and end apart: 7 -> 7, of which waited for: 5 -> 6; matrix products, arithmetic and copies ran while one was open for 6% -> 5% of each run, Pallas kernels for 23% -> 23%
where the time goes in v7:
time: 501 us; the launch traced here: 499 us
  waiting for transfers between devices  277 us (55%)
  Pallas kernels  116 us (23%)
  local copies, waits for them, and re-layouts  46.4 us (9%)
  starting transfers between devices  33.1 us (7%)
  other arithmetic  25 us (5%)
    all_to_all x4, waiting for transfers between devices, per_device_body(): lax.all_to_all(payload, 'seq', split_axis=0, concat_axis=0, tiled=True)  123 us
    pallas_call x4, Pallas kernels, attend(): pl.pallas_call(attention_kernel, grid_spec=grid_spec, out_shape=jax.Shape...  105 us
    all_to_all x1, waiting for transfers between devices, per_device_body(): lax.all_to_all(value_payload, 'seq', split_axis=0, concat_axis=0, tiled=T...  89.4 us
    all_to_all x2, waiting for transfers between devices, per_device_body(): lax.all_to_all(group, 'seq', split_axis=0, concat_axis=0, tiled=True)  65.5 us
    unnamed x54, local copies, waits for them, and re-layouts  40 us
    all_to_all x4, starting transfers between devices, per_device_body(): lax.all_to_all(payload, 'seq', split_axis=0, concat_axis=0, tiled=True)  19.1 us
    concatenate x4, other arithmetic, per_device_body(): jnp.concatenate([by_destination(array, heads) for array in normed], axis=1)  10.2 us
  transfers between devices with their start and end apart: 7, of which 6 were waited for; matrix products, arithmetic and copies ran while one was open for 5% of the time, Pallas kernels for 23%

profile of v7, /device:TPU:0, one launch (start us, length us, event | category | flops | bytes accessed | tf_op | source)
XLA Modules:
  0.0 499.0 jit_solution(8228241861426101387)
XLA Ops:
  0.6 3.3 copy.33
  3.9 4.1 copy.35
  8.0 2.6 fusion.6
  10.7 2.4 fusion.8
  18.5 3.3 copy.37
  21.7 4.1 copy.39
  25.8 2.6 fusion.11
  28.5 2.4 fusion.13
  37.0 2.9 pad_maximum_fusion.2
  40.0 7.3 %all-to-all-start.3 = ((bf16[8,4,256,128]{3,2,1,0:T(8,128)(2,1)}), bf16[8,4,256,128]{3,2,1,0:T(8,128)(2,1)S(1)}, u32[]{:S(2)}, u32[]{:S(2)}) async-start(bf16[8,4,256,128]{3,2,1,0:T(8,128)(2,1)} %pad_maximum_fusion.2), calls=%async_computation.3 | async-start | bytes 4194304 | tf_op jit(solution)/shard_map/all_to_all | solution.py:265
  55.5 3.1 pad_maximum_fusion.3
  58.6 37.0 %all-to-all-done.3.q_ref.dq_ref.k_ref.dk_ref = bf16[8,4,256,128]{3,2,1,0:T(8,128)(2,1)S(1)} async-done(((bf16[8,4,256,128]{3,2,1,0:T(8,128)(2,1)}), bf16[8,4,256,128]{3,2,1,0:T(8,128)(2,1)S(1)}, u32[]{:S(2)}, u32[]{:S(2)}) %all-to-all-start.3) | async-done | bytes 2097184 | tf_op jit(solution)/shard_map/all_to_all | solution.py:265
  96.9 4.3 all-to-all-start.4
  105.3 2.6 pad_maximum_fusion.4
  107.9 41.1 %all-to-all-done.4.q_ref.dq_ref.k_ref.dk_ref = bf16[8,4,256,128]{3,2,1,0:T(8,128)(2,1)} async-done(((bf16[8,4,256,128]{3,2,1,0:T(8,128)(2,1)}), bf16[8,4,256,128]{3,2,1,0:T(8,128)(2,1)}, u32[]{:S(2)}, u32[]{:S(2)}) %all-to-all-start.4) | async-done | bytes 2097184 | tf_op jit(solution)/shard_map/all_to_all | solution.py:265
  149.0 3.6 all-to-all-start.5
  152.7 3.9 shard_map.104
  156.6 44.5 %all-to-all-done.5.q_ref.dq_ref.k_ref.dk_ref = bf16[8,4,256,128]{3,2,1,0:T(8,128)(2,1)S(1)} async-done(((bf16[8,4,256,128]{3,2,1,0:T(8,128)(2,1)}), bf16[8,4,256,128]{3,2,1,0:T(8,128)(2,1)S(1)}, u32[]{:S(2)}, u32[]{:S(2)}) %all-to-all-start.5) | async-done | bytes 2097184 | tf_op jit(solution)/shard_map/all_to_all | solution.py:265
  202.5 4.6 all-to-all-start.1
  210.2 89.4 %all-to-all-done.1.v_ref.dv_ref = bf16[8,8,256,128]{3,2,1,0:T(8,128)(2,1)} async-done(((bf16[8,8,256,128]{3,2,1,0:T(8,128)(2,1)}), bf16[8,8,256,128]{3,2,1,0:T(8,128)(2,1)}, u32[]{:S(2)}, u32[]{:S(2)}) %all-to-all-start.1) | async-done | bytes 4194336 | tf_op jit(solution)/shard_map/all_to_all | solution.py:254
  299.6 3.8 all-to-all-start
  305.6 26.2 %shard_map.108 = bf16[8,2,256,128]{3,2,1,0:T(8,128)(2,1)} custom-call(s32[8]{0:T(128)} %get-tuple-element.14.first_ref, s32[8]{0:T(128)} %get-tuple-element.13.last_ref, s32[4]{0:T(128)} %bitcast.28, bf16[8,4,256,128]{3,2,1,0:T(8,128)(2,1)} %copy-done.2, bf16[8,4,256,128]{3,2,1,0:T(8,128)(2,1)} %copy-done.2, bf16[8,4,256,128]{3,2,1,0:T(8,128)(2,1)} %copy-done.2, ...), custom_call_target="tpu_custom_call" | custom-call | tf_op jit(solution)/shard_map/pallas_call | solution.py:143
  331.8 26.2 %shard_map.107 = bf16[8,2,256,128]{3,2,1,0:T(8,128)(2,1)} custom-call(s32[8]{0:T(128)} %get-tuple-element.14.first_ref, s32[8]{0:T(128)} %get-tuple-element.13.last_ref, s32[4]{0:T(128)} %bitcast.29, bf16[8,4,256,128]{3,2,1,0:T(8,128)(2,1)} %all-to-all-done.4.q_ref.dq_ref.k_ref.dk_ref, bf16[8,4,256,128]{3,2,1,0:T(8,128)(2,1)} %all-to-all-done.4.q_ref.dq_ref.k_ref.dk_ref, ...), custom_call_target="tpu_custom_call" | custom-call | tf_op jit(solution)/shard_map/pallas_call | solution.py:143
  358.0 26.3 %shard_map.106 = bf16[8,2,256,128]{3,2,1,0:T(8,128)(2,1)} custom-call(s32[8]{0:T(128)} %get-tuple-element.14.first_ref, s32[8]{0:T(128)} %get-tuple-element.13.last_ref, s32[4]{0:T(128)} %bitcast.30, bf16[8,4,256,128]{3,2,1,0:T(8,128)(2,1)} %copy-done.1, bf16[8,4,256,128]{3,2,1,0:T(8,128)(2,1)} %copy-done.1, bf16[8,4,256,128]{3,2,1,0:T(8,128)(2,1)} %copy-done.1, ...), custom_call_target="tpu_custom_call" | custom-call | tf_op jit(solution)/shard_map/pallas_call | solution.py:143
  384.4 3.7 pad_maximum_fusion
  389.4 5.8 %all-to-all-start.6 = ((bf16[8,2,256,384]{3,2,1,0:T(8,128)(2,1)}), bf16[8,2,256,384]{3,2,1,0:T(8,128)(2,1)}, u32[]{:S(2)}, u32[]{:S(2)}) async-start(bf16[8,2,256,384]{3,2,1,0:T(8,128)(2,1)} %pad_maximum_fusion), calls=%async_computation.6 | async-start | bytes 6291456 | tf_op jit(solution)/shard_map/all_to_all | solution.py:277
  395.2 26.2 %shard_map.105 = bf16[8,2,256,128]{3,2,1,0:T(8,128)(2,1)} custom-call(s32[8]{0:T(128)} %get-tuple-element.14.first_ref, s32[8]{0:T(128)} %get-tuple-element.13.last_ref, s32[4]{0:T(128)} %bitcast.31, bf16[8,4,256,128]{3,2,1,0:T(8,128)(2,1)} %copy-done.3, bf16[8,4,256,128]{3,2,1,0:T(8,128)(2,1)} %copy-done.3, bf16[8,4,256,128]{3,2,1,0:T(8,128)(2,1)} %copy-done.3, ...), custom_call_target="tpu_custom_call" | custom-call | tf_op jit(solution)/shard_map/pallas_call | solution.py:143
  421.4 44.2 %all-to-all-done.6.received_ref = bf16[8,2,256,384]{3,2,1,0:T(8,128)(2,1)} async-done(((bf16[8,2,256,384]{3,2,1,0:T(8,128)(2,1)}), bf16[8,2,256,384]{3,2,1,0:T(8,128)(2,1)}, u32[]{:S(2)}, u32[]{:S(2)}) %all-to-all-start.6) | async-done | bytes 3145760 | tf_op jit(solution)/shard_map/all_to_all | solution.py:277
  465.6 3.6 all-to-all-start.2
  469.2 4.7 shard_map.109
  474.0 21.2 %all-to-all-done.2.received_ref = bf16[8,2,256,128]{3,2,1,0:T(8,128)(2,1)S(1)} async-done(((bf16[8,2,256,128]{3,2,1,0:T(8,128)(2,1)}), bf16[8,2,256,128]{3,2,1,0:T(8,128)(2,1)S(1)}, u32[]{:S(2)}, u32[]{:S(2)}) %all-to-all-start.2) | async-done | bytes 1048608 | tf_op jit(solution)/shard_map/all_to_all | solution.py:277
  496.2 2.7 shard_map.110
  (70 shorter events, 34.2 us)
Async XLA Ops:
  8.0 2.6 copy-start.4
  8.0 2.7 copy-start.14
  13.1 2.2 copy-start.6
  25.8 2.6 copy-start.5
  25.8 2.7 copy-start.15
  30.9 3.4 copy-start.7
  40.0 55.5 %all-to-all-start.3 = ((bf16[8,4,256,128]{3,2,1,0:T(8,128)(2,1)}), bf16[8,4,256,128]{3,2,1,0:T(8,128)(2,1)S(1)}, u32[]{:S(2)}, u32[]{:S(2)}) async-start(bf16[8,4,256,128]{3,2,1,0:T(8,128)(2,1)} %pad_maximum_fusion.2), calls=%async_computation.3 | async-start | bytes 4194304 | tf_op jit(solution)/shard_map/all_to_all | solution.py:265
  95.5 1.3 copy-start.1
  96.9 52.2 %all-to-all-start.4 = ((bf16[8,4,256,128]{3,2,1,0:T(8,128)(2,1)}), bf16[8,4,256,128]{3,2,1,0:T(8,128)(2,1)}, u32[]{:S(2)}, u32[]{:S(2)}) async-start(bf16[8,4,256,128]{3,2,1,0:T(8,128)(2,1)} %pad_maximum_fusion.3), calls=%async_computation.4 | async-start | bytes 4194304 | tf_op jit(solution)/shard_map/all_to_all | solution.py:265
  101.2 2.7 copy-start.13
  101.2 3.8 copy-start.12
  149.0 52.0 %all-to-all-start.5 = ((bf16[8,4,256,128]{3,2,1,0:T(8,128)(2,1)}), bf16[8,4,256,128]{3,2,1,0:T(8,128)(2,1)S(1)}, u32[]{:S(2)}, u32[]{:S(2)}) async-start(bf16[8,4,256,128]{3,2,1,0:T(8,128)(2,1)} %pad_maximum_fusion.4), calls=%async_computation.5 | async-start | bytes 4194304 | tf_op jit(solution)/shard_map/all_to_all | solution.py:265
  201.1 1.4 copy-start.2
  202.5 97.1 %all-to-all-start.1 = ((bf16[8,8,256,128]{3,2,1,0:T(8,128)(2,1)}), bf16[8,8,256,128]{3,2,1,0:T(8,128)(2,1)}, u32[]{:S(2)}, u32[]{:S(2)}) async-start(bf16[8,8,256,128]{3,2,1,0:T(8,128)(2,1)} %shard_map.104), calls=%async_computation.1 | async-start | bytes 8388608 | tf_op jit(solution)/shard_map/all_to_all | solution.py:254
  207.0 1.0 copy-start.11
  207.0 1.3 copy-start.10
  210.2 93.2 %copy-start.16 = (s32[2,4]{1,0:T(2,128)S(1)}, s32[2,4]{1,0:T(2,128)}, u32[]{:S(2)}) copy-start(s32[2,4]{1,0:T(2,128)} %param.19) | copy-start | bytes 100
  299.6 88.5 %all-to-all-start = ((bf16[8,4,256,128]{3,2,1,0:T(8,128)(2,1)}), bf16[8,4,256,128]{3,2,1,0:T(8,128)(2,1)S(1)}, u32[]{:S(2)}, u32[]{:S(2)}) async-start(bf16[8,4,256,128]{3,2,1,0:T(8,128)(2,1)} %pad_maximum_fusion.1), calls=%async_computation | async-start | bytes 4194304 | tf_op jit(solution)/shard_map/all_to_all | solution.py:265
  303.6 2.0 copy-start
  358.0 26.3 %copy-start.9 = (bf16[8,2,256,128]{3,2,1,0:T(8,128)(2,1)S(1)}, bf16[8,2,256,128]{3,2,1,0:T(8,128)(2,1)}, u32[]{:S(2)}) copy-start(bf16[8,2,256,128]{3,2,1,0:T(8,128)(2,1)} %shard_map.108) | copy-start | bytes 3145732
  388.1 1.3 copy-start.3
  389.4 76.2 %all-to-all-start.6 = ((bf16[8,2,256,384]{3,2,1,0:T(8,128)(2,1)}), bf16[8,2,256,384]{3,2,1,0:T(8,128)(2,1)}, u32[]{:S(2)}, u32[]{:S(2)}) async-start(bf16[8,2,256,384]{3,2,1,0:T(8,128)(2,1)} %pad_maximum_fusion), calls=%async_computation.6 | async-start | bytes 6291456 | tf_op jit(solution)/shard_map/all_to_all | solution.py:277
  465.6 29.6 %all-to-all-start.2 = ((bf16[8,2,256,128]{3,2,1,0:T(8,128)(2,1)}), bf16[8,2,256,128]{3,2,1,0:T(8,128)(2,1)S(1)}, u32[]{:S(2)}, u32[]{:S(2)}) async-start(bf16[8,2,256,128]{3,2,1,0:T(8,128)(2,1)} %shard_map.105), calls=%async_computation.2 | async-start | bytes 2097152 | tf_op jit(solution)/shard_map/all_to_all | solution.py:277
  495.2 1.0 copy-start.8
